TPU v7x, 256 devices: a whole 4x4x8 slice. The times are simulated.
256 devices in a mesh: rep: 16 (over x_hi, z), fsdp: 16 (over x_lo, y, core).
Axes of the slice: x: 4 (x_hi: 2, x_lo: 2; x = x_hi * 2 + x_lo), y: 4, z: 8, core: 2. Of those that a mesh axis runs over, the one named last changes fastest.
Arguments:
- outer_start: float32 [2048, 8192], P(None, 'fsdp'), may hold values from -6 to 6
- local_weights: bfloat16 [16, 2048, 8192], P('rep', None, 'fsdp'), may hold values from -9 to 9
- momentum: float32 [2048, 8192], P('rep', 'fsdp'), may hold values from -0.6 to 0.6
Outputs:
- new_weights: bfloat16 [2048, 8192], P(None, 'fsdp')
- new_master: float32 [2048, 8192], P('rep', 'fsdp')
- new_momentum: float32 [2048, 8192], P('rep', 'fsdp')
All inputs are finite; a program needn't handle non-finite values.
Results may differ from a plain program's by a relative error of at most 0.0045.
Values may be sent and summed in bfloat16 or wider, within the bound.
No kernel may reach another device: no remote copies, remote signals or barrier semaphores. Data moves between devices by JAX's collectives and lax.ppermute only.
A program may use at most 64 MiB of HBM per device.

v0:
```python
import jax
import jax.numpy as jnp
from jax import lax
from jax.sharding import PartitionSpec as P

D = 8192


clip_level = 0.03
outer_rate = 0.7
momentum_coef = 0.9
eps_value = 1e-06


def make_difference(outer_rows, local_rows):
    rounded = (outer_rows - local_rows.astype(jnp.float32)).astype(jnp.bfloat16)
    rounded = lax.optimization_barrier(rounded)
    return rounded.astype(jnp.float32)


def outer_update(own_outer, outer_grad, unit_squares, momentum_rows):
    factor = jnp.minimum(1.0, clip_level / jnp.sqrt(unit_squares / D + eps_value))
    clipped = outer_grad * factor[:, None]
    new_momentum = momentum_coef * momentum_rows + clipped
    new_master = own_outer - outer_rate * (clipped + momentum_coef * new_momentum)
    return (new_master, new_momentum)


def on_device(outer_start, local_weights, momentum):
    local_shard = local_weights[0]
    replicas = lax.axis_size("rep")
    owner = lax.axis_index("rep")
    own_rows = outer_start.shape[0] // replicas
    summed = lax.psum_scatter(
        make_difference(outer_start, local_shard).astype(jnp.bfloat16),
        "rep",
        scatter_dimension=0,
        tiled=True,
    ).astype(jnp.float32)
    own_outer = lax.dynamic_slice_in_dim(outer_start, owner * own_rows, own_rows, 0)
    outer_grad = summed / replicas
    unit_squares = lax.psum(jnp.sum(outer_grad * outer_grad, axis=1), "fsdp")
    new_master, new_momentum = outer_update(own_outer, outer_grad, unit_squares, momentum)
    new_weights = lax.all_gather(new_master.astype(jnp.bfloat16), "rep", axis=0, tiled=True)
    return (new_weights, new_master, new_momentum)


def solution(mesh):
    return jax.shard_map(
        on_device,
        mesh=mesh,
        in_specs=(P(None, "fsdp"), P("rep", None, "fsdp"), P("rep", "fsdp")),
        out_specs=(P(None, "fsdp"), P("rep", "fsdp"), P("rep", "fsdp")),
        check_vma=False,
    )
```

profile of v0, /device:TPU:4, one launch (start us, length us, event | category | flops | bytes accessed | tf_op | source)
XLA Modules:
  0.0 342.4 jit_solution(3331967806520791519)
XLA Ops:
  7.2 0.0 reduce-scatter.2.cloned.1.call-start
  7.2 4.9 %fusion = bf16[2048,512]{1,0:T(8,128)(2,1)} fusion(f32[2048,512]{1,0:T(8,128)} %param.3, bf16[1,2048,512]{2,1,0:T(8,128)(2,1)} %param.4), kind=kLoop, calls=%fused_computation.1 | loop fusion | flops 3145728 | bytes 8388608 | tf_op jit(solution)/shard_map/convert_element_type | solution.py:16
  12.1 0.0 copy-start
  12.1 0.0 reduce-scatter.2.cloned.1.call-update
  12.1 0.0 all-gather.2.cloned.1.call-start
  12.2 210.1 %reduce-scatter.2.cloned.1.call-done = bf16[128,512]{1,0:T(8,128)(2,1)} async-done(((bf16[2048,512]{1,0:T(8,128)(2,1)}), bf16[128,512]{1,0:T(8,128)(2,1)}) %reduce-scatter.2.cloned.1.call-update) | async-done | bytes 131088 | tf_op jit(solution)/shard_map/reduce_scatter | solution.py:34
  222.3 1.0 fusion.6
  223.3 27.1 %psum.7 = f32[128]{0:T(128)S(1)} all-reduce(f32[128]{0:T(128)S(1)} %fusion.6), channel_id=1, replica_groups=mesh['rep'=16,'fsdp'=16] {'fsdp'}, use_global_device_ids=true, to_apply=%region_2.0 | all-reduce | flops 128 | bytes 1024 | tf_op jit(solution)/shard_map/psum | solution.py:42
  250.5 0.0 copy-done
  250.5 2.0 fusion.7
  252.5 0.0 all-gather.2.cloned.1.call-update
  252.5 80.1 %all-gather.2.cloned.1.call-done = bf16[2048,512]{1,0:T(8,128)(2,1)} async-done(((bf16[128,512]{1,0:T(8,128)(2,1)}), bf16[2048,512]{1,0:T(8,128)(2,1)}) %all-gather.2.cloned.1.call-update) | async-done | bytes 2097168 | tf_op jit(solution)/shard_map/all_gather | solution.py:44
  332.5 3.0 copy.7
  (1 shorter events, 0.0 us)
Async XLA Ops:
  7.2 215.1 %reduce-scatter.2.cloned.1.call-start = ((), (), s32[]{:S(2)}) async-start(), calls=%async_computation.1 | async-start | bytes 2228224 | tf_op jit(solution)/shard_map/reduce_scatter | solution.py:34
  12.1 238.4 %copy-start = (f32[128,512]{1,0:T(8,128)S(1)}, f32[128,512]{1,0:T(8,128)}, u32[]{:S(2)}) copy-start(f32[128,512]{1,0:T(8,128)} %param.5) | copy-start | bytes 786436
  12.1 320.4 %all-gather.2.cloned.1.call-start = ((), (), s32[]{:S(2)}) async-start(), calls=%async_computation.2 | async-start | bytes 2228224 | tf_op jit(solution)/shard_map/all_gather | solution.py:44
Sparse Core Ops, SparseCore 0:
  12.5 209.7 reduce-scatter.1
  252.6 79.8 all-gather.1
where the time goes:
time: 345 us; the launch traced here: 342 us
  waiting for transfers between devices  290 us (84%)
  blocking collectives  27.1 us (8%)
  between operations  14 us (4%)
  other arithmetic  7.92 us (2%)
    reduce_scatter x1, waiting for transfers between devices, on_device(): lax.psum_scatter(make_difference(outer_start, local_shard).astype(jnp.bfl...  210 us
    all_gather x1, waiting for transfers between devices, on_device(): lax.all_gather(new_master.astype(jnp.bfloat16), 'rep', axis=0, tiled=True)  80.1 us
    psum x1, blocking collectives, on_device(): unit_squares = lax.psum(jnp.sum(outer_grad * outer_grad, axis=1), 'fsdp')  27.1 us
  transfers between devices with their start and end apart: 2, of which 2 were waited for; matrix products, arithmetic and copies ran while one was open for 0% of the time, Pallas kernels for 0%

commit v1 on v0

v1 whole, which is shorter than its diff:
```python
import jax
import jax.numpy as jnp
from jax import lax
from jax.sharding import PartitionSpec as P

D = 8192
clip_level = 0.03
outer_rate = 0.7
momentum_coef = 0.9
eps_value = 1e-06


def outer_update(own_outer, outer_grad, unit_squares, momentum_rows):
    factor = jnp.minimum(1.0, clip_level / jnp.sqrt(unit_squares / D + eps_value))
    clipped = outer_grad * factor[:, None]
    new_momentum = momentum_coef * momentum_rows + clipped
    new_master = own_outer - outer_rate * (clipped + momentum_coef * new_momentum)
    return (new_master, new_momentum)


def rs_psum_scatter(diff):
    return lax.psum_scatter(diff, "rep", scatter_dimension=0, tiled=True).astype(jnp.float32)


def rs_a2a(diff):
    n = lax.axis_size("rep")
    x = diff.reshape(n, diff.shape[0] // n, diff.shape[1])
    y = lax.all_to_all(x, "rep", 0, 0, tiled=False)
    return jnp.sum(y.astype(jnp.float32), axis=0)


def ag_all_gather(w):
    return lax.all_gather(w, "rep", axis=0, tiled=True)


def ag_a2a(w):
    n = lax.axis_size("rep")
    x = jnp.broadcast_to(w[None], (n,) + w.shape)
    y = lax.all_to_all(x, "rep", 0, 0, tiled=False)
    return y.reshape(n * w.shape[0], w.shape[1])


def sq_psum(s):
    return lax.psum(s, "fsdp")


def sq_a2a(s):
    n = lax.axis_size("fsdp")
    x = jnp.broadcast_to(s[None], (n,) + s.shape)
    y = lax.all_to_all(x, "fsdp", 0, 0, tiled=False)
    return jnp.sum(y, axis=0)


def sq_ag(s):
    return jnp.sum(lax.all_gather(s, "fsdp", axis=0, tiled=False), axis=0)


def make(rs, sq, ag):
    def on_device(outer_start, local_weights, momentum):
        local_shard = local_weights[0]
        replicas = lax.axis_size("rep")
        owner = lax.axis_index("rep")
        own_rows = outer_start.shape[0] // replicas
        diff = (outer_start - local_shard.astype(jnp.float32)).astype(jnp.bfloat16)
        summed = rs(diff)
        own_outer = lax.dynamic_slice_in_dim(outer_start, owner * own_rows, own_rows, 0)
        outer_grad = summed / replicas
        unit_squares = sq(jnp.sum(outer_grad * outer_grad, axis=1))
        new_master, new_momentum = outer_update(own_outer, outer_grad, unit_squares, momentum)
        new_weights = ag(new_master.astype(jnp.bfloat16))
        return (new_weights, new_master, new_momentum)

    def solution(mesh):
        return jax.shard_map(
            on_device,
            mesh=mesh,
            in_specs=(P(None, "fsdp"), P("rep", None, "fsdp"), P("rep", "fsdp")),
            out_specs=(P(None, "fsdp"), P("rep", "fsdp"), P("rep", "fsdp")),
            check_vma=False,
        )
    return solution
solution = make(rs_a2a, sq_a2a, ag_a2a)
```

time: 345 us -> 136 us (0.39)
  waiting for transfers between devices: 290 us -> 5.97 us
  blocking collectives: 27.1 us -> 115 us
  between operations: 14 us -> 0.67 us
  starting transfers between devices: 0.08 us -> 5.21 us
    reduce_scatter x1 -> x0, waiting for transfers between devices: 210 us -> none  [on_device(): lax.psum_scatter(make_difference(outer_start, local_shard).astype(jnp.bfl...]
    all_to_all x0 -> x2, blocking collectives: none -> 115 us  [the longest x1 59.4 us: rs_a2a(): y = lax.all_to_all(x, 'rep', 0, 0, tiled=False)]
    all_gather x1 -> x0, waiting for transfers between devices: 80.1 us -> none  [on_device(): lax.all_gather(new_master.astype(jnp.bfloat16), 'rep', axis=0, tiled=True)]
    psum x1 -> x0, blocking collectives: 27.1 us -> none  [on_device(): unit_squares = lax.psum(jnp.sum(outer_grad * outer_grad, axis=1), 'fsdp')]
    all_to_all x0 -> x1, waiting for transfers between devices: none -> 5.97 us  [sq_a2a(): y = lax.all_to_all(x, 'fsdp', 0, 0, tiled=False)]
    all_to_all x0 -> x1, starting transfers between devices: none -> 5.21 us  [sq_a2a(): y = lax.all_to_all(x, 'fsdp', 0, 0, tiled=False)]
  transfers between devices with their start and end apart: 2 -> 1, of which waited for: 2 -> 1; matrix products, arithmetic and copies ran while one was open for 0% -> 0% of each run, Pallas kernels for 0% -> 0%
where the time goes in v1:
time: 136 us; the launch traced here: 135 us
  blocking collectives  115 us (85%)
  waiting for transfers between devices  5.97 us (4%)
  other arithmetic  5.89 us (4%)
  starting transfers between devices  5.21 us (4%)
  local copies, waits for them, and re-layouts  2.13 us (2%)
    all_to_all x1, blocking collectives, rs_a2a(): y = lax.all_to_all(x, 'rep', 0, 0, tiled=False)  59.4 us
    all_to_all x1, blocking collectives, ag_a2a(): y = lax.all_to_all(x, 'rep', 0, 0, tiled=False)  55.3 us
    all_to_all x1, waiting for transfers between devices, sq_a2a(): y = lax.all_to_all(x, 'fsdp', 0, 0, tiled=False)  5.97 us
    all_to_all x1, starting transfers between devices, sq_a2a(): y = lax.all_to_all(x, 'fsdp', 0, 0, tiled=False)  5.21 us
    convert_element_type x1, other arithmetic, on_device(): diff = (outer_start - local_shard.astype(jnp.float32)).astype(jnp.bfloat16)  3.59 us
  transfers between devices with their start and end apart: 1, of which 1 were waited for; matrix products, arithmetic and copies ran while one was open for 0% of the time, Pallas kernels for 0%

profile of v1, /device:TPU:4, one launch (start us, length us, event | category | flops | bytes accessed | tf_op | source)
XLA Modules:
  0.0 134.5 jit_solution(12041803051212651167)
XLA Ops:
  0.6 3.6 %fusion = bf16[2048,512]{1,0:T(8,128)(2,1)S(1)} fusion(f32[2048,512]{1,0:T(8,128)} %param.3, bf16[1,2048,512]{2,1,0:T(8,128)(2,1)} %param.4), kind=kLoop, calls=%fused_computation.1 | loop fusion | flops 3145728 | bytes 8388608 | tf_op jit(solution)/shard_map/convert_element_type | solution.py:64
  4.2 59.4 %all_to_all.16 = bf16[16,128,512]{2,1,0:T(8,128)(2,1)S(1)} all-to-all(bf16[16,128,512]{2,1,0:T(8,128)(2,1)S(1)} %bitcast.7), channel_id=1, replica_groups=mesh['rep'=16,'fsdp'=16] {'rep'}, dimensions={0} | all-to-all | bytes 4194304 | tf_op jit(solution)/shard_map/all_to_all | solution.py:28
  63.6 0.0 copy-start
  63.6 0.3 convert_reduce_fusion
  63.9 0.1 multiply_reduce_fusion
  64.0 0.6 broadcast_in_dim.4
  64.7 5.2 %all-to-all-start.1 = ((f32[16,1,128]{2,1,0:T(1,128)}), f32[16,1,128]{2,1,0:T(1,128)S(1)}, u32[]{:S(2)}, u32[]{:S(2)}) async-start(f32[16,1,128]{2,1,0:T(1,128)} %broadcast_in_dim.4), calls=%async_computation.1 | async-start | bytes 16384 | tf_op jit(solution)/shard_map/all_to_all | solution.py:50
  69.9 6.0 %all-to-all-done.1 = f32[16,1,128]{2,1,0:T(1,128)S(1)} async-done(((f32[16,1,128]{2,1,0:T(1,128)}), f32[16,1,128]{2,1,0:T(1,128)S(1)}, u32[]{:S(2)}, u32[]{:S(2)}) %all-to-all-start.1) | async-done | bytes 8224 | tf_op jit(solution)/shard_map/all_to_all | solution.py:50
  75.9 0.0 copy-done
  75.9 1.9 %fusion.1 = (bf16[128,512]{1,0:T(8,128)(2,1)S(1)}, f32[128,512]{1,0:T(8,128)}, f32[128,512]{1,0:T(8,128)}) fusion(f32[128,512]{1,0:T(8,128)S(1)} %convert_reduce_fusion, f32[128]{0:T(128)S(1)} %minimum_multiply_fusion, f32[2048,512]{1,0:T(8,128)} %param.3, s32[]{:T(128)S(6)} %select_n.3, f32[128,512]{1,0:T(8,128)S(1)} %copy-done), kind=kLoop, calls=%fused_computation.7 | loop fusion | flops 524288 | bytes 1442308 | tf_op jit(solution)/shard_map/convert_element_type | solution.py:70
  77.8 0.2 broadcast_in_dim.5
  78.0 55.3 %all_to_all.17 = bf16[16,128,512]{2,1,0:T(8,128)(2,1)S(1)} all-to-all(bf16[16,128,512]{2,1,0:T(8,128)(2,1)S(1)} %broadcast_in_dim.5), channel_id=1, replica_groups=mesh['rep'=16,'fsdp'=16] {'rep'}, dimensions={0} | all-to-all | bytes 4194304 | tf_op jit(solution)/shard_map/all_to_all | solution.py:39
  133.2 1.3 copy.8
  (2 shorter events, 0.0 us)
Async XLA Ops:
  63.6 12.2 %copy-start = (f32[128,512]{1,0:T(8,128)S(1)}, f32[128,512]{1,0:T(8,128)}, u32[]{:S(2)}) copy-start(f32[128,512]{1,0:T(8,128)} %param.5) | copy-start | bytes 786436
  64.7 11.2 %all-to-all-start.1 = ((f32[16,1,128]{2,1,0:T(1,128)}), f32[16,1,128]{2,1,0:T(1,128)S(1)}, u32[]{:S(2)}, u32[]{:S(2)}) async-start(f32[16,1,128]{2,1,0:T(1,128)} %broadcast_in_dim.4), calls=%async_computation.1 | async-start | bytes 16384 | tf_op jit(solution)/shard_map/all_to_all | solution.py:50

commit v2 on v1

--- a/solution.py
+++ b/solution.py
@@ -79,4 +79,62 @@
             check_vma=False,
         )
     return solution
-solution = make(rs_a2a, sq_a2a, ag_a2a)
+
+NX = 2
+
+
+def _perms(n):
+    nz = n // NX
+    cw = [(x * nz + k, x * nz + (k + 1) % nz) for x in range(NX) for k in range(nz)]
+    ccw = [(x * nz + k, x * nz + (k - 1) % nz) for x in range(NX) for k in range(nz)]
+    xp = [(x * nz + k, (1 - x) * nz + k) for x in range(NX) for k in range(nz)]
+    return nz, cw, ccw, xp
+
+
+def rs_ring4(diff):
+    n = lax.axis_size("rep")
+    nz, cw, ccw, xp = _perms(n)
+    r = lax.axis_index("rep")
+    xh, z = r // nz, r % nz
+    rows = diff.shape[0] // n
+    t = diff.reshape(NX, nz, rows, diff.shape[1])
+    take = lambda i: lax.dynamic_index_in_dim(t, i % nz, 1, keepdims=False)
+    n_cw, n_ccw = nz // 2, (nz - 1) // 2
+    send_cw, send_ccw = take(z + n_cw), take(z - n_ccw)
+    for s in range(n_cw):
+        got_cw = lax.ppermute(send_cw, "rep", cw)
+        if s < n_ccw:
+            got_ccw = lax.ppermute(send_ccw, "rep", ccw)
+        if s < n_cw - 1:
+            send_cw = (got_cw.astype(jnp.float32) + take(z + n_cw - 1 - s).astype(jnp.float32)).astype(jnp.bfloat16)
+        if s < n_ccw - 1:
+            send_ccw = (got_ccw.astype(jnp.float32) + take(z - n_ccw + 1 + s).astype(jnp.float32)).astype(jnp.bfloat16)
+    own = take(z).astype(jnp.float32) + got_cw.astype(jnp.float32) + got_ccw.astype(jnp.float32)
+    first = xh == 0
+    mine = jnp.where(first, own[0], own[1])
+    other = jnp.where(first, own[1], own[0]).astype(jnp.bfloat16)
+    return mine + lax.ppermute(other, "rep", xp).astype(jnp.float32)
+
+
+def ag_ring4(w):
+    n = lax.axis_size("rep")
+    nz, cw, ccw, xp = _perms(n)
+    r = lax.axis_index("rep")
+    xh, z = r // nz, r % nz
+    wx = lax.ppermute(w, "rep", xp)
+    first = xh == 0
+    blk = jnp.stack([jnp.where(first, w, wx), jnp.where(first, wx, w)])
+    n_cw, n_ccw = nz // 2, (nz - 1) // 2
+    cur_cw, cur_ccw = blk, blk
+    got_cw, got_ccw = [], []
+    for s in range(n_cw):
+        cur_cw = lax.ppermute(cur_cw, "rep", cw)
+        got_cw.append(cur_cw)
+        if s < n_ccw:
+            cur_ccw = lax.ppermute(cur_ccw, "rep", ccw)
+            got_ccw.append(cur_ccw)
+    by_offset = [blk] + got_ccw + got_cw[::-1]
+    stacked = jnp.stack(by_offset, axis=1)
+    out = jnp.roll(stacked, z, axis=1)
+    return out.reshape(n * w.shape[0], w.shape[1])
+solution = make(rs_ring4, sq_a2a, ag_ring4)

time: 136 us -> 104 us (0.76); the launches traced: 135 us -> 104 us
  blocking collectives: 115 us -> 0 us
  waiting for transfers between devices: 5.97 us -> 63.6 us
  starting transfers between devices: 5.21 us -> 29.1 us
  other arithmetic: 5.89 us -> 7.83 us
    all_to_all x2 -> x0, blocking collectives: 115 us -> none  [the longest x1 59.4 us: rs_a2a(): y = lax.all_to_all(x, 'rep', 0, 0, tiled=False)]
    ppermute x0 -> x16, waiting for transfers between devices: none -> 57.6 us  [the longest x4 24.1 us: rs_ring4(): got_cw = lax.ppermute(send_cw, 'rep', cw)]
    ppermute x0 -> x16, starting transfers between devices: none -> 23.9 us  [the longest x3 10.5 us: rs_ring4(): got_ccw = lax.ppermute(send_ccw, 'rep', ccw)]
    convert_element_type x0 -> x4, other arithmetic: none -> 2.01 us  [the longest x3 1.99 us: rs_ring4(): (got_cw.astype(jnp.float32) + take(z + n_cw - 1 - s).astype(jnp.float32))...]
    dynamic_slice x0 -> x2, local copies, waits for them, and re-layouts: none -> 1.72 us  [ag_ring4(): out = jnp.roll(stacked, z, axis=1)]
  transfers between devices with their start and end apart: 1 -> 17, of which waited for: 1 -> 11; matrix products, arithmetic and copies ran while one was open for 0% -> 1% of each run, Pallas kernels for 0% -> 0%
where the time goes in v2:
time: 104 us
  waiting for transfers between devices  63.6 us (61%)
  starting transfers between devices  29.1 us (28%)
  other arithmetic  7.83 us (8%)
  local copies, waits for them, and re-layouts  2.64 us (3%)
    ppermute x4, waiting for transfers between devices, rs_ring4(): got_cw = lax.ppermute(send_cw, 'rep', cw)  24.1 us
    ppermute x4, waiting for transfers between devices, ag_ring4(): cur_cw = lax.ppermute(cur_cw, 'rep', cw)  21.6 us
    ppermute x3, starting transfers between devices, rs_ring4(): got_ccw = lax.ppermute(send_ccw, 'rep', ccw)  10.5 us
    ppermute x3, starting transfers between devices, ag_ring4(): cur_ccw = lax.ppermute(cur_ccw, 'rep', ccw)  7.05 us
    all_to_all x1, waiting for transfers between devices, sq_a2a(): y = lax.all_to_all(x, 'fsdp', 0, 0, tiled=False)  5.98 us
    ppermute x1, waiting for transfers between devices, rs_ring4(): return mine + lax.ppermute(other, 'rep', xp).astype(jnp.float32)  5.97 us
    ppermute x1, waiting for transfers between devices, ag_ring4(): wx = lax.ppermute(w, 'rep', xp)  5.95 us
    all_to_all x1, starting transfers between devices, sq_a2a(): y = lax.all_to_all(x, 'fsdp', 0, 0, tiled=False)  5.21 us
  transfers between devices with their start and end apart: 17, of which 11 were waited for; matrix products, arithmetic and copies ran while one was open for 1% of the time, Pallas kernels for 0%

profile of v2, /device:TPU:4, one launch (start us, length us, event | category | flops | bytes accessed | tf_op | source)
XLA Modules:
  0.0 104.1 jit_solution(8838238392833566911)
XLA Ops:
  0.7 3.6 %fusion = bf16[2048,512]{1,0:T(8,128)(2,1)S(1)} fusion(f32[2048,512]{1,0:T(8,128)} %param.3, bf16[1,2048,512]{2,1,0:T(8,128)(2,1)} %param.4), kind=kLoop, calls=%fused_computation.1 | loop fusion | flops 3145728 | bytes 8388608 | tf_op jit(solution)/shard_map/convert_element_type | solution.py:64
  4.3 0.0 copy-start
  4.3 2.0 %collective-permute-start = (bf16[2,128,512]{2,1,0:T(8,128)(2,1)S(1)}, bf16[2,128,512]{2,1,0:T(8,128)(2,1)}, u32[]{:S(2)}, u32[]{:S(2)}) collective-permute-start(bf16[2,128,512]{2,1,0:T(8,128)(2,1)S(1)} %get-tuple-element.12), channel_id=1, source_target_pairs={{0,16},{16,32},{32,48},{48,64},{64,80},{80,96},{96,112},{112,0},{1... | collective-permute-start | bytes 786440 | tf_op jit(solution)/shard_map/ppermute | solution.py:105
  6.3 4.0 %collective-permute-start.4 = (bf16[2,128,512]{2,1,0:T(8,128)(2,1)S(1)}, bf16[2,128,512]{2,1,0:T(8,128)(2,1)S(1)}, u32[]{:S(2)}, u32[]{:S(2)}) collective-permute-start(bf16[2,128,512]{2,1,0:T(8,128)(2,1)S(1)} %get-tuple-element.13), channel_id=1, source_target_pairs={{0,112},{16,0},{32,16},{48,32},{64,48},{80,64},{96,80},{112,96},{1... | collective-permute-start | bytes 786440 | tf_op jit(solution)/shard_map/ppermute | solution.py:107
  10.4 6.3 %collective-permute-done = bf16[2,128,512]{2,1,0:T(8,128)(2,1)} collective-permute-done((bf16[2,128,512]{2,1,0:T(8,128)(2,1)S(1)}, bf16[2,128,512]{2,1,0:T(8,128)(2,1)}, u32[]{:S(2)}, u32[]{:S(2)}) %collective-permute-start) | collective-permute-done | bytes 262176 | tf_op jit(solution)/shard_map/ppermute | solution.py:105
  16.7 1.0 fusion.5
  17.7 0.1 collective-permute-start.1
  17.8 0.0 collective-permute-done.4
  17.8 8.6 %collective-permute-done.1 = bf16[2,128,512]{2,1,0:T(8,128)(2,1)S(1)} collective-permute-done((bf16[2,128,512]{2,1,0:T(8,128)(2,1)S(1)}, bf16[2,128,512]{2,1,0:T(8,128)(2,1)S(1)}, u32[]{:S(2)}, u32[]{:S(2)}) %collective-permute-start.1) | collective-permute-done | bytes 262176 | tf_op jit(solution)/shard_map/ppermute | solution.py:105
  26.5 0.1 fusion.4
  26.6 0.1 collective-permute-start.2
  26.7 3.2 %collective-permute-start.5 = (bf16[2,128,512]{2,1,0:T(8,128)(2,1)S(1)}, bf16[2,128,512]{2,1,0:T(8,128)(2,1)S(1)}, u32[]{:S(2)}, u32[]{:S(2)}) collective-permute-start(bf16[2,128,512]{2,1,0:T(8,128)(2,1)S(1)} %get-tuple-element.11), channel_id=1, source_target_pairs={{0,112},{16,0},{32,16},{48,32},{64,48},{80,64},{96,80},{112,96},{1... | collective-permute-start | bytes 786440 | tf_op jit(solution)/shard_map/ppermute | solution.py:107
  29.9 4.5 %collective-permute-done.2 = bf16[2,128,512]{2,1,0:T(8,128)(2,1)S(1)} collective-permute-done((bf16[2,128,512]{2,1,0:T(8,128)(2,1)S(1)}, bf16[2,128,512]{2,1,0:T(8,128)(2,1)S(1)}, u32[]{:S(2)}, u32[]{:S(2)}) %collective-permute-start.2) | collective-permute-done | bytes 262176 | tf_op jit(solution)/shard_map/ppermute | solution.py:105
  34.5 0.0 collective-permute-done.5
  34.5 0.8 fusion.3
  35.3 0.0 collective-permute-start.3
  35.3 3.2 %collective-permute-start.6 = (bf16[2,128,512]{2,1,0:T(8,128)(2,1)S(1)}, bf16[2,128,512]{2,1,0:T(8,128)(2,1)S(1)}, u32[]{:S(2)}, u32[]{:S(2)}) collective-permute-start(bf16[2,128,512]{2,1,0:T(8,128)(2,1)S(1)} %get-tuple-element.9), channel_id=1, source_target_pairs={{0,112},{16,0},{32,16},{48,32},{64,48},{80,64},{96,80},{112,96},{1... | collective-permute-start | bytes 786440 | tf_op jit(solution)/shard_map/ppermute | solution.py:107
  38.6 4.6 %collective-permute-done.3 = bf16[2,128,512]{2,1,0:T(8,128)(2,1)S(1)} collective-permute-done((bf16[2,128,512]{2,1,0:T(8,128)(2,1)}, bf16[2,128,512]{2,1,0:T(8,128)(2,1)S(1)}, u32[]{:S(2)}, u32[]{:S(2)}) %collective-permute-start.3) | collective-permute-done | bytes 262176 | tf_op jit(solution)/shard_map/ppermute | solution.py:105
  43.1 0.0 collective-permute-done.6
  43.1 0.1 fusion.6
  43.3 0.6 collective-permute-start.7
  43.9 6.0 %collective-permute-done.7 = bf16[128,512]{1,0:T(8,128)(2,1)S(1)} collective-permute-done((bf16[128,512]{1,0:T(8,128)(2,1)S(1)}, bf16[128,512]{1,0:T(8,128)(2,1)S(1)}, u32[]{:S(2)}, u32[]{:S(2)}) %collective-permute-start.7) | collective-permute-done | bytes 131104 | tf_op jit(solution)/shard_map/ppermute | solution.py:116
  49.8 0.1 multiply_reduce_fusion
  50.0 0.6 broadcast_in_dim.2
  50.6 5.2 %all-to-all-start = ((f32[16,1,128]{2,1,0:T(1,128)}), f32[16,1,128]{2,1,0:T(1,128)S(1)}, u32[]{:S(2)}, u32[]{:S(2)}) async-start(f32[16,1,128]{2,1,0:T(1,128)} %broadcast_in_dim.2), calls=%async_computation | async-start | bytes 16384 | tf_op jit(solution)/shard_map/all_to_all | solution.py:50
  55.8 6.0 %all-to-all-done = f32[16,1,128]{2,1,0:T(1,128)S(1)} async-done(((f32[16,1,128]{2,1,0:T(1,128)}), f32[16,1,128]{2,1,0:T(1,128)S(1)}, u32[]{:S(2)}, u32[]{:S(2)}) %all-to-all-start) | async-done | bytes 8224 | tf_op jit(solution)/shard_map/all_to_all | solution.py:50
  61.8 0.0 copy-done
  61.8 1.9 %fusion.8 = (bf16[128,512]{1,0:T(8,128)(2,1)S(1)}, f32[128,512]{1,0:T(8,128)}, f32[128,512]{1,0:T(8,128)}) fusion(f32[128,512]{1,0:T(8,128)S(1)} %get-tuple-element.7, f32[128]{0:T(128)S(1)} %minimum_multiply_fusion, f32[2048,512]{1,0:T(8,128)} %param.3, s32[]{:T(128)S(6)} %select_n.114, f32[128,512]{1,0:T(8,128)S(1)} %copy-done), kind=kLoop, calls=%fused_computation.43 | loop fusion | flops 524288 | bytes 1442308 | tf_op jit(solution)/shard_map/convert_element_type | solution.py:70
  63.7 0.8 collective-permute-start.8
  64.5 5.9 %collective-permute-done.8 = bf16[128,512]{1,0:T(8,128)(2,1)S(1)} collective-permute-done((bf16[128,512]{1,0:T(8,128)(2,1)S(1)}, bf16[128,512]{1,0:T(8,128)(2,1)S(1)}, u32[]{:S(2)}, u32[]{:S(2)}) %collective-permute-start.8) | collective-permute-done | bytes 131104 | tf_op jit(solution)/shard_map/ppermute | solution.py:124
  70.5 2.1 %collective-permute-start.12 = (bf16[2,128,512]{2,1,0:T(8,128)(2,1)S(1)}, bf16[2,128,512]{2,1,0:T(8,128)(2,1)S(1)}, u32[]{:S(2)}, u32[]{:S(2)}) collective-permute-start(bf16[2,128,512]{2,1,0:T(8,128)(2,1)S(1)} %pad_maximum_fusion), channel_id=1, source_target_pairs={{0,16},{16,32},{32,48},{48,64},{64,80},{80,96},{96,112},{112,0},{1... | collective-permute-start | bytes 786440 | tf_op jit(solution)/shard_map/ppermute | solution.py:131
  72.6 1.2 %collective-permute-start.9 = (bf16[2,128,512]{2,1,0:T(8,128)(2,1)S(1)}, bf16[2,128,512]{2,1,0:T(8,128)(2,1)S(1)}, u32[]{:S(2)}, u32[]{:S(2)}) collective-permute-start(bf16[2,128,512]{2,1,0:T(8,128)(2,1)S(1)} %pad_maximum_fusion), channel_id=1, source_target_pairs={{0,112},{16,0},{32,16},{48,32},{64,48},{80,64},{96,80},{112,96},{1... | collective-permute-start | bytes 786440 | tf_op jit(solution)/shard_map/ppermute | solution.py:134
  73.8 5.2 %collective-permute-done.12 = bf16[2,128,512]{2,1,0:T(8,128)(2,1)S(1)} collective-permute-done((bf16[2,128,512]{2,1,0:T(8,128)(2,1)S(1)}, bf16[2,128,512]{2,1,0:T(8,128)(2,1)S(1)}, u32[]{:S(2)}, u32[]{:S(2)}) %collective-permute-start.12) | collective-permute-done | bytes 262176 | tf_op jit(solution)/shard_map/ppermute | solution.py:131
  79.0 0.7 collective-permute-start.13
  79.7 0.0 collective-permute-done.9
  79.7 2.5 %collective-permute-start.10 = (bf16[2,128,512]{2,1,0:T(8,128)(2,1)S(1)}, bf16[2,128,512]{2,1,0:T(8,128)(2,1)S(1)}, u32[]{:S(2)}, u32[]{:S(2)}) collective-permute-start(bf16[2,128,512]{2,1,0:T(8,128)(2,1)S(1)} %collective-permute-done.9), channel_id=1, source_target_pairs={{0,112},{16,0},{32,16},{48,32},{64,48},{80,64},{96,80},{112,96},{1... | collective-permute-start | bytes 786440 | tf_op jit(solution)/shard_map/ppermute | solution.py:134
  82.3 4.3 %collective-permute-done.13 = bf16[2,128,512]{2,1,0:T(8,128)(2,1)S(1)} collective-permute-done((bf16[2,128,512]{2,1,0:T(8,128)(2,1)S(1)}, bf16[2,128,512]{2,1,0:T(8,128)(2,1)S(1)}, u32[]{:S(2)}, u32[]{:S(2)}) %collective-permute-start.13) | collective-permute-done | bytes 262176 | tf_op jit(solution)/shard_map/ppermute | solution.py:131
  86.6 0.0 collective-permute-start.14
  86.6 0.0 collective-permute-done.10
  86.6 3.3 %collective-permute-start.11 = (bf16[2,128,512]{2,1,0:T(8,128)(2,1)S(1)}, bf16[2,128,512]{2,1,0:T(8,128)(2,1)S(1)}, u32[]{:S(2)}, u32[]{:S(2)}) collective-permute-start(bf16[2,128,512]{2,1,0:T(8,128)(2,1)S(1)} %collective-permute-done.10), channel_id=1, source_target_pairs={{0,112},{16,0},{32,16},{48,32},{64,48},{80,64},{96,80},{112,96},{1... | collective-permute-start | bytes 786440 | tf_op jit(solution)/shard_map/ppermute | solution.py:134
  90.0 4.5 %collective-permute-done.14 = bf16[2,128,512]{2,1,0:T(8,128)(2,1)S(1)} collective-permute-done((bf16[2,128,512]{2,1,0:T(8,128)(2,1)S(1)}, bf16[2,128,512]{2,1,0:T(8,128)(2,1)S(1)}, u32[]{:S(2)}, u32[]{:S(2)}) %collective-permute-start.14) | collective-permute-done | bytes 262176 | tf_op jit(solution)/shard_map/ppermute | solution.py:131
  94.5 0.0 collective-permute-start.15
  94.5 0.0 collective-permute-done.11
  94.6 7.5 %collective-permute-done.15 = bf16[2,128,512]{2,1,0:T(8,128)(2,1)S(1)} collective-permute-done((bf16[2,128,512]{2,1,0:T(8,128)(2,1)S(1)}, bf16[2,128,512]{2,1,0:T(8,128)(2,1)S(1)}, u32[]{:S(2)}, u32[]{:S(2)}) %collective-permute-start.15) | collective-permute-done | bytes 262176 | tf_op jit(solution)/shard_map/ppermute | solution.py:131
  102.4 0.2 constant_dynamic-slice_fusion
  102.6 1.5 %copy.24 = bf16[2,8,128,512]{3,2,1,0:T(8,128)(2,1)} copy(bf16[2,8,128,512]{3,2,0,1:T(8,128)(2,1)S(1)} %constant_dynamic-slice_fusion) | data formatting | bytes 4194304 | tf_op jit(solution)/shard_map/jit(_roll_dynamic)/dynamic_slice | solution.py:138
  (22 shorter events, 0.5 us)
Async XLA Ops:
  4.3 57.5 %copy-start = (f32[128,512]{1,0:T(8,128)S(1)}, f32[128,512]{1,0:T(8,128)}, u32[]{:S(2)}) copy-start(f32[128,512]{1,0:T(8,128)} %param.5) | copy-start | bytes 786436
  4.3 12.3 %collective-permute-start = (bf16[2,128,512]{2,1,0:T(8,128)(2,1)S(1)}, bf16[2,128,512]{2,1,0:T(8,128)(2,1)}, u32[]{:S(2)}, u32[]{:S(2)}) collective-permute-start(bf16[2,128,512]{2,1,0:T(8,128)(2,1)S(1)} %get-tuple-element.12), channel_id=1, source_target_pairs={{0,16},{16,32},{32,48},{48,64},{64,80},{80,96},{96,112},{112,0},{1... | collective-permute-start | bytes 786440 | tf_op jit(solution)/shard_map/ppermute | solution.py:105
  6.3 11.5 %collective-permute-start.4 = (bf16[2,128,512]{2,1,0:T(8,128)(2,1)S(1)}, bf16[2,128,512]{2,1,0:T(8,128)(2,1)S(1)}, u32[]{:S(2)}, u32[]{:S(2)}) collective-permute-start(bf16[2,128,512]{2,1,0:T(8,128)(2,1)S(1)} %get-tuple-element.13), channel_id=1, source_target_pairs={{0,112},{16,0},{32,16},{48,32},{64,48},{80,64},{96,80},{112,96},{1... | collective-permute-start | bytes 786440 | tf_op jit(solution)/shard_map/ppermute | solution.py:107
  17.7 8.8 %collective-permute-start.1 = (bf16[2,128,512]{2,1,0:T(8,128)(2,1)S(1)}, bf16[2,128,512]{2,1,0:T(8,128)(2,1)S(1)}, u32[]{:S(2)}, u32[]{:S(2)}) collective-permute-start(bf16[2,128,512]{2,1,0:T(8,128)(2,1)S(1)} %fusion.5), channel_id=1, source_target_pairs={{0,16},{16,32},{32,48},{48,64},{64,80},{80,96},{96,112},{112,0},{1... | collective-permute-start | bytes 786440 | tf_op jit(solution)/shard_map/ppermute | solution.py:105
  26.6 7.9 %collective-permute-start.2 = (bf16[2,128,512]{2,1,0:T(8,128)(2,1)S(1)}, bf16[2,128,512]{2,1,0:T(8,128)(2,1)S(1)}, u32[]{:S(2)}, u32[]{:S(2)}) collective-permute-start(bf16[2,128,512]{2,1,0:T(8,128)(2,1)S(1)} %get-tuple-element.10), channel_id=1, source_target_pairs={{0,16},{16,32},{32,48},{48,64},{64,80},{80,96},{96,112},{112,0},{1... | collective-permute-start | bytes 786440 | tf_op jit(solution)/shard_map/ppermute | solution.py:105
  26.7 7.8 %collective-permute-start.5 = (bf16[2,128,512]{2,1,0:T(8,128)(2,1)S(1)}, bf16[2,128,512]{2,1,0:T(8,128)(2,1)S(1)}, u32[]{:S(2)}, u32[]{:S(2)}) collective-permute-start(bf16[2,128,512]{2,1,0:T(8,128)(2,1)S(1)} %get-tuple-element.11), channel_id=1, source_target_pairs={{0,112},{16,0},{32,16},{48,32},{64,48},{80,64},{96,80},{112,96},{1... | collective-permute-start | bytes 786440 | tf_op jit(solution)/shard_map/ppermute | solution.py:107
  35.3 7.8 %collective-permute-start.3 = (bf16[2,128,512]{2,1,0:T(8,128)(2,1)}, bf16[2,128,512]{2,1,0:T(8,128)(2,1)S(1)}, u32[]{:S(2)}, u32[]{:S(2)}) collective-permute-start(bf16[2,128,512]{2,1,0:T(8,128)(2,1)} %get-tuple-element.8), channel_id=1, source_target_pairs={{0,16},{16,32},{32,48},{48,64},{64,80},{80,96},{96,112},{112,0},{1... | collective-permute-start | bytes 786440 | tf_op jit(solution)/shard_map/ppermute | solution.py:105
  35.3 7.8 %collective-permute-start.6 = (bf16[2,128,512]{2,1,0:T(8,128)(2,1)S(1)}, bf16[2,128,512]{2,1,0:T(8,128)(2,1)S(1)}, u32[]{:S(2)}, u32[]{:S(2)}) collective-permute-start(bf16[2,128,512]{2,1,0:T(8,128)(2,1)S(1)} %get-tuple-element.9), channel_id=1, source_target_pairs={{0,112},{16,0},{32,16},{48,32},{64,48},{80,64},{96,80},{112,96},{1... | collective-permute-start | bytes 786440 | tf_op jit(solution)/shard_map/ppermute | solution.py:107
  43.3 6.6 %collective-permute-start.7 = (bf16[128,512]{1,0:T(8,128)(2,1)S(1)}, bf16[128,512]{1,0:T(8,128)(2,1)S(1)}, u32[]{:S(2)}, u32[]{:S(2)}) collective-permute-start(bf16[128,512]{1,0:T(8,128)(2,1)S(1)} %fusion.7), channel_id=1, source_target_pairs={{0,128},{16,144},{32,160},{48,176},{64,192},{80,208},{96,224},{112... | collective-permute-start | bytes 393224 | tf_op jit(solution)/shard_map/ppermute | solution.py:116
  50.6 11.2 %all-to-all-start = ((f32[16,1,128]{2,1,0:T(1,128)}), f32[16,1,128]{2,1,0:T(1,128)S(1)}, u32[]{:S(2)}, u32[]{:S(2)}) async-start(f32[16,1,128]{2,1,0:T(1,128)} %broadcast_in_dim.2), calls=%async_computation | async-start | bytes 16384 | tf_op jit(solution)/shard_map/all_to_all | solution.py:50
  63.7 6.7 %collective-permute-start.8 = (bf16[128,512]{1,0:T(8,128)(2,1)S(1)}, bf16[128,512]{1,0:T(8,128)(2,1)S(1)}, u32[]{:S(2)}, u32[]{:S(2)}) collective-permute-start(bf16[128,512]{1,0:T(8,128)(2,1)S(1)} %get-tuple-element.3), channel_id=1, source_target_pairs={{0,128},{16,144},{32,160},{48,176},{64,192},{80,208},{96,224},{112... | collective-permute-start | bytes 393224 | tf_op jit(solution)/shard_map/ppermute | solution.py:124
  70.5 8.5 %collective-permute-start.12 = (bf16[2,128,512]{2,1,0:T(8,128)(2,1)S(1)}, bf16[2,128,512]{2,1,0:T(8,128)(2,1)S(1)}, u32[]{:S(2)}, u32[]{:S(2)}) collective-permute-start(bf16[2,128,512]{2,1,0:T(8,128)(2,1)S(1)} %pad_maximum_fusion), channel_id=1, source_target_pairs={{0,16},{16,32},{32,48},{48,64},{64,80},{80,96},{96,112},{112,0},{1... | collective-permute-start | bytes 786440 | tf_op jit(solution)/shard_map/ppermute | solution.py:131
  72.6 7.2 %collective-permute-start.9 = (bf16[2,128,512]{2,1,0:T(8,128)(2,1)S(1)}, bf16[2,128,512]{2,1,0:T(8,128)(2,1)S(1)}, u32[]{:S(2)}, u32[]{:S(2)}) collective-permute-start(bf16[2,128,512]{2,1,0:T(8,128)(2,1)S(1)} %pad_maximum_fusion), channel_id=1, source_target_pairs={{0,112},{16,0},{32,16},{48,32},{64,48},{80,64},{96,80},{112,96},{1... | collective-permute-start | bytes 786440 | tf_op jit(solution)/shard_map/ppermute | solution.py:134
  79.0 7.6 %collective-permute-start.13 = (bf16[2,128,512]{2,1,0:T(8,128)(2,1)S(1)}, bf16[2,128,512]{2,1,0:T(8,128)(2,1)S(1)}, u32[]{:S(2)}, u32[]{:S(2)}) collective-permute-start(bf16[2,128,512]{2,1,0:T(8,128)(2,1)S(1)} %collective-permute-done.12), channel_id=1, source_target_pairs={{0,16},{16,32},{32,48},{48,64},{64,80},{80,96},{96,112},{112,0},{1... | collective-permute-start | bytes 786440 | tf_op jit(solution)/shard_map/ppermute | solution.py:131
  79.7 6.9 %collective-permute-start.10 = (bf16[2,128,512]{2,1,0:T(8,128)(2,1)S(1)}, bf16[2,128,512]{2,1,0:T(8,128)(2,1)S(1)}, u32[]{:S(2)}, u32[]{:S(2)}) collective-permute-start(bf16[2,128,512]{2,1,0:T(8,128)(2,1)S(1)} %collective-permute-done.9), channel_id=1, source_target_pairs={{0,112},{16,0},{32,16},{48,32},{64,48},{80,64},{96,80},{112,96},{1... | collective-permute-start | bytes 786440 | tf_op jit(solution)/shard_map/ppermute | solution.py:134
  86.6 7.9 %collective-permute-start.14 = (bf16[2,128,512]{2,1,0:T(8,128)(2,1)S(1)}, bf16[2,128,512]{2,1,0:T(8,128)(2,1)S(1)}, u32[]{:S(2)}, u32[]{:S(2)}) collective-permute-start(bf16[2,128,512]{2,1,0:T(8,128)(2,1)S(1)} %collective-permute-done.13), channel_id=1, source_target_pairs={{0,16},{16,32},{32,48},{48,64},{64,80},{80,96},{96,112},{112,0},{1... | collective-permute-start | bytes 786440 | tf_op jit(solution)/shard_map/ppermute | solution.py:131
  86.6 7.9 %collective-permute-start.11 = (bf16[2,128,512]{2,1,0:T(8,128)(2,1)S(1)}, bf16[2,128,512]{2,1,0:T(8,128)(2,1)S(1)}, u32[]{:S(2)}, u32[]{:S(2)}) collective-permute-start(bf16[2,128,512]{2,1,0:T(8,128)(2,1)S(1)} %collective-permute-done.10), channel_id=1, source_target_pairs={{0,112},{16,0},{32,16},{48,32},{64,48},{80,64},{96,80},{112,96},{1... | collective-permute-start | bytes 786440 | tf_op jit(solution)/shard_map/ppermute | solution.py:134
  94.5 7.6 %collective-permute-start.15 = (bf16[2,128,512]{2,1,0:T(8,128)(2,1)S(1)}, bf16[2,128,512]{2,1,0:T(8,128)(2,1)S(1)}, u32[]{:S(2)}, u32[]{:S(2)}) collective-permute-start(bf16[2,128,512]{2,1,0:T(8,128)(2,1)S(1)} %collective-permute-done.14), channel_id=1, source_target_pairs={{0,16},{16,32},{32,48},{48,64},{64,80},{80,96},{96,112},{112,0},{1... | collective-permute-start | bytes 786440 | tf_op jit(solution)/shard_map/ppermute | solution.py:131

commit v3 on v0

v3 whole, which is shorter than its diff:
```python
import jax
import jax.numpy as jnp
from jax import lax
from jax.sharding import PartitionSpec as P

D = 8192
NX = 2

clip_level = 0.03
outer_rate = 0.7
momentum_coef = 0.9
eps_value = 1e-06


def outer_update(own_outer, outer_grad, unit_squares, momentum_rows):
    factor = jnp.minimum(1.0, clip_level / jnp.sqrt(unit_squares / D + eps_value))
    clipped = outer_grad * factor[:, None]
    new_momentum = momentum_coef * momentum_rows + clipped
    new_master = own_outer - outer_rate * (clipped + momentum_coef * new_momentum)
    return (new_master, new_momentum)


def ring_perms(n):
    nz = n // NX
    cw = [(x * nz + k, x * nz + (k + 1) % nz) for x in range(NX) for k in range(nz)]
    ccw = [(x * nz + k, x * nz + (k - 1) % nz) for x in range(NX) for k in range(nz)]
    xp = [(x * nz + k, (1 - x) * nz + k) for x in range(NX) for k in range(nz)]
    return nz, cw, ccw, xp


def f32(x):
    return x.astype(jnp.float32)


def reduce_scatter(term, n):
    nz, cw, ccw, xp = ring_perms(n)
    r = lax.axis_index("rep")
    xh, z = r // nz, r % nz
    steps = nz // 2
    half = term(z).shape[-1] // 2
    send_cw = term(z + steps)[..., :half]
    send_ccw = term(z - steps)[..., half:]
    for s in range(steps):
        got_cw = lax.ppermute(send_cw, "rep", cw)
        got_ccw = lax.ppermute(send_ccw, "rep", ccw)
        if s == steps - 1:
            break
        own_cw = f32(term(z + steps - 1 - s))
        own_ccw = f32(term(z - steps + 1 + s))
        if s == 0:
            send_cw = jnp.concatenate([f32(got_cw) + own_cw[..., :half], own_cw[..., half:]], axis=-1)
            send_ccw = jnp.concatenate([own_ccw[..., :half], f32(got_ccw) + own_ccw[..., half:]], axis=-1)
        else:
            send_cw = f32(got_cw) + own_cw
            send_ccw = f32(got_ccw) + own_ccw
        send_cw = send_cw.astype(jnp.bfloat16)
        send_ccw = send_ccw.astype(jnp.bfloat16)
    total = (f32(term(z)) + f32(got_cw) + f32(got_ccw)).astype(jnp.bfloat16)
    return f32(total) + f32(lax.ppermute(total, "rep", xp))


def all_gather(w, n):
    nz, cw, ccw, xp = ring_perms(n)
    r = lax.axis_index("rep")
    xh, z = r // nz, r % nz
    blk = w
    rows, cols = w.shape[1:]
    half = cols // 2
    out = jnp.zeros((NX, nz, rows, cols), w.dtype)
    put = lambda o, piece, pos, col: lax.dynamic_update_slice(o, piece[:, None], (0, pos % nz, 0, col))
    out = put(out, blk, z, 0)
    steps = nz // 2
    cur_cw, cur_ccw = blk, blk
    for s in range(steps):
        if s == steps - 1:
            cur_cw = cur_cw[..., :half]
            cur_ccw = cur_ccw[..., half:]
        cur_cw = lax.ppermute(cur_cw, "rep", cw)
        cur_ccw = lax.ppermute(cur_ccw, "rep", ccw)
        out = put(out, cur_cw, z - 1 - s, 0)
        out = put(out, cur_ccw, z + 1 + s, half if s == steps - 1 else 0)
    return out.reshape(n * rows, cols)


def on_device(outer_start, local_weights, momentum):
    local_shard = local_weights[0]
    replicas = lax.axis_size("rep")
    owner = lax.axis_index("rep")
    own_rows = outer_start.shape[0] // replicas
    cols = outer_start.shape[1]
    nz = replicas // NX
    start_blocks = outer_start.reshape(NX, nz, own_rows, cols)
    local_blocks = local_shard.reshape(NX, nz, own_rows, cols)

    def term(i):
        i = i % nz
        a = lax.dynamic_index_in_dim(start_blocks, i, 1, keepdims=False)
        b = lax.dynamic_index_in_dim(local_blocks, i, 1, keepdims=False)
        return (a - b.astype(jnp.float32)).astype(jnp.bfloat16)

    xh = owner // nz
    first = xh == 0
    partner_momentum = lax.ppermute(momentum, "rep", ring_perms(replicas)[3])
    both_momentum = jnp.stack([jnp.where(first, momentum, partner_momentum), jnp.where(first, partner_momentum, momentum)])
    summed = reduce_scatter(term, replicas)
    both_outer = lax.dynamic_index_in_dim(start_blocks, owner % nz, 1, keepdims=False)
    outer_grad = summed / replicas
    partial = jnp.sum(outer_grad * outer_grad, axis=2)
    shards = lax.axis_size("fsdp")
    spread = jnp.broadcast_to(partial[None], (shards,) + partial.shape)
    unit_squares = jnp.sum(lax.all_to_all(spread, "fsdp", 0, 0, tiled=False), axis=0)
    factor = jnp.minimum(1.0, clip_level / jnp.sqrt(unit_squares / D + eps_value))
    clipped = outer_grad * factor[..., None]
    both_new_momentum = momentum_coef * both_momentum + clipped
    both_new_master = both_outer - outer_rate * (clipped + momentum_coef * both_new_momentum)
    new_weights = all_gather(both_new_master.astype(jnp.bfloat16), replicas)
    new_master = lax.dynamic_index_in_dim(both_new_master, xh, 0, keepdims=False)
    new_momentum = lax.dynamic_index_in_dim(both_new_momentum, xh, 0, keepdims=False)
    return (new_weights, new_master, new_momentum)


def solution(mesh):
    return jax.shard_map(
        on_device,
        mesh=mesh,
        in_specs=(P(None, "fsdp"), P("rep", None, "fsdp"), P("rep", "fsdp")),
        out_specs=(P(None, "fsdp"), P("rep", "fsdp"), P("rep", "fsdp")),
        check_vma=False,
    )
```

time: 345 us -> 97.8 us (0.28)
  waiting for transfers between devices: 290 us -> 46.5 us
  starting transfers between devices: 0.08 us -> 38 us
  blocking collectives: 27.1 us -> 0 us
  between operations: 14 us -> 0.98 us
    reduce_scatter x1 -> x0, waiting for transfers between devices: 210 us -> none  [on_device(): lax.psum_scatter(make_difference(outer_start, local_shard).astype(jnp.bfl...]
    all_gather x1 -> x0, waiting for transfers between devices: 80.1 us -> none  [on_device(): lax.all_gather(new_master.astype(jnp.bfloat16), 'rep', axis=0, tiled=True)]
    ppermute x0 -> x18, waiting for transfers between devices: none -> 40.4 us  [the longest x4 17.6 us: reduce_scatter(): got_cw = lax.ppermute(send_cw, 'rep', cw)]
    ppermute x0 -> x18, starting transfers between devices: none -> 32.8 us  [the longest x4 11.7 us: reduce_scatter(): got_ccw = lax.ppermute(send_ccw, 'rep', ccw)]
    psum x1 -> x0, blocking collectives: 27.1 us -> none  [on_device(): unit_squares = lax.psum(jnp.sum(outer_grad * outer_grad, axis=1), 'fsdp')]
    all_to_all x0 -> x1, waiting for transfers between devices: none -> 6.02 us  [on_device(): lax.all_to_all(spread, 'fsdp', 0, 0, tiled=False)]
    all_to_all x0 -> x1, starting transfers between devices: none -> 5.21 us  [on_device(): lax.all_to_all(spread, 'fsdp', 0, 0, tiled=False)]
  transfers between devices with their start and end apart: 2 -> 19, of which waited for: 2 -> 11; matrix products, arithmetic and copies ran while one was open for 0% -> 3% of each run, Pallas kernels for 0% -> 0%
where the time goes in v3:
time: 97.8 us; the launch traced here: 97.5 us
  waiting for transfers between devices  46.5 us (48%)
  starting transfers between devices  38 us (39%)
  other arithmetic  8.07 us (8%)
  local copies, waits for them, and re-layouts  3.99 us (4%)
  between operations  0.98 us (1%)
    ppermute x4, waiting for transfers between devices, reduce_scatter(): got_cw = lax.ppermute(send_cw, 'rep', cw)  17.6 us
    ppermute x4, waiting for transfers between devices, all_gather(): cur_cw = lax.ppermute(cur_cw, 'rep', cw)  17.4 us
    ppermute x4, starting transfers between devices, reduce_scatter(): got_ccw = lax.ppermute(send_ccw, 'rep', ccw)  11.7 us
    ppermute x4, starting transfers between devices, all_gather(): cur_ccw = lax.ppermute(cur_ccw, 'rep', ccw)  10.3 us
    all_to_all x1, waiting for transfers between devices, on_device(): lax.all_to_all(spread, 'fsdp', 0, 0, tiled=False)  6.02 us
    all_to_all x1, starting transfers between devices, on_device(): lax.all_to_all(spread, 'fsdp', 0, 0, tiled=False)  5.21 us
    ppermute x1, waiting for transfers between devices, reduce_scatter(): return f32(total) + f32(lax.ppermute(total, 'rep', xp))  4.47 us
    ppermute x4, starting transfers between devices, reduce_scatter(): got_cw = lax.ppermute(send_cw, 'rep', cw)  4.34 us
  transfers between devices with their start and end apart: 19, of which 11 were waited for; matrix products, arithmetic and copies ran while one was open for 3% of the time, Pallas kernels for 0%

profile of v3, /device:TPU:4, one launch (start us, length us, event | category | flops | bytes accessed | tf_op | source)
XLA Modules:
  0.0 97.5 jit_solution(10902890050908957455)
XLA Ops:
  0.7 2.2 %fusion.18 = (bf16[2,128,512]{2,1,0:T(8,128)(2,1)S(1)}, bf16[2,128,512]{2,1,0:T(8,128)(2,1)S(1)}, bf16[2,128,512]{2,1,0:T(8,128)(2,1)S(1)}, bf16[2,128,512]{2,1,0:T(8,128)(2,1)S(1)}) fusion(f32[2,8,128,512]{3,2,1,0:T(8,128)} %bitcast.139, s32[]{:T(128)S(6)} %select_n.141, bf16[2,8,128,512]{3,2,1,0:T(8,128)(2,1)} %bitcast.144, s32[]{:T(128)S(6)} %select_n.151, ...), kind=kLoop, calls=%fused_computation.36 | loop fusion | flops 1572864 | bytes 4194320 | tf_op jit(solution)/shard_map/convert_element_type | solution.py:99
  2.9 0.0 copy-start
  2.9 2.0 %collective-permute-start = (bf16[2,128,256]{2,1,0:T(8,128)(2,1)S(1)}, bf16[2,128,256]{2,1,0:T(8,128)(2,1)S(1)}, u32[]{:S(2)}, u32[]{:S(2)}) collective-permute-start(bf16[2,128,256]{2,1,0:T(8,128)(2,1)S(1)} %slice.42), channel_id=1, source_target_pairs={{0,16},{16,32},{32,48},{48,64},{64,80},{80,96},{96,112},{112,0},{1... | collective-permute-start | bytes 393224 | tf_op jit(solution)/shard_map/ppermute | solution.py:44
  5.0 4.0 %collective-permute-start.4 = (bf16[2,128,256]{2,1,0:T(8,128)(2,1)S(1)}, bf16[2,128,256]{2,1,0:T(8,128)(2,1)S(1)}, u32[]{:S(2)}, u32[]{:S(2)}) collective-permute-start(bf16[2,128,256]{2,1,0:T(8,128)(2,1)S(1)} %slice.46), channel_id=1, source_target_pairs={{0,112},{16,0},{32,16},{48,32},{64,48},{80,64},{96,80},{112,96},{1... | collective-permute-start | bytes 393224 | tf_op jit(solution)/shard_map/ppermute | solution.py:45
  9.0 3.4 %collective-permute-done = bf16[2,128,256]{2,1,0:T(8,128)(2,1)S(1)} collective-permute-done((bf16[2,128,256]{2,1,0:T(8,128)(2,1)S(1)}, bf16[2,128,256]{2,1,0:T(8,128)(2,1)S(1)}, u32[]{:S(2)}, u32[]{:S(2)}) %collective-permute-start) | collective-permute-done | bytes 131104 | tf_op jit(solution)/shard_map/ppermute | solution.py:44
  12.4 0.1 collective-permute-start.1
  12.6 3.3 %collective-permute-start.5 = (bf16[2,128,512]{2,1,0:T(8,128)(2,1)S(1)}, bf16[2,128,512]{2,1,0:T(8,128)(2,1)S(1)}, u32[]{:S(2)}, u32[]{:S(2)}) collective-permute-start(bf16[2,128,512]{2,1,0:T(8,128)(2,1)S(1)} %pad_maximum_fusion.1), channel_id=1, source_target_pairs={{0,112},{16,0},{32,16},{48,32},{64,48},{80,64},{96,80},{112,96},{1... | collective-permute-start | bytes 786440 | tf_op jit(solution)/shard_map/ppermute | solution.py:45
  15.9 5.3 %collective-permute-done.1 = bf16[2,128,512]{2,1,0:T(8,128)(2,1)S(1)} collective-permute-done((bf16[2,128,512]{2,1,0:T(8,128)(2,1)S(1)}, bf16[2,128,512]{2,1,0:T(8,128)(2,1)S(1)}, u32[]{:S(2)}, u32[]{:S(2)}) %collective-permute-start.1) | collective-permute-done | bytes 262176 | tf_op jit(solution)/shard_map/ppermute | solution.py:44
  21.2 1.4 %fusion.12 = (bf16[2,128,512]{2,1,0:T(8,128)(2,1)S(1)}, bf16[2,128,512]{2,1,0:T(8,128)(2,1)S(1)}) fusion(bf16[2,128,512]{2,1,0:T(8,128)(2,1)S(1)} %collective-permute-done.1, f32[2,8,128,512]{3,2,1,0:T(8,128)} %bitcast.140, s32[]{:T(128)S(6)} %select_n.145, bf16[2,8,128,512]{3,2,1,0:T(8,128)(2,1)S(1)} %bitcast.145, s32[]{:T(128)S(6)} %select_n.153, ...), kind=kLoop, calls=%fused_computation.25 | loop fusion | flops 1835008 | bytes 2621448 | tf_op jit(solution)/shard_map/convert_element_type | solution.py:56
  22.7 0.1 collective-permute-start.2
  22.7 3.2 %collective-permute-start.6 = (bf16[2,128,512]{2,1,0:T(8,128)(2,1)S(1)}, bf16[2,128,512]{2,1,0:T(8,128)(2,1)S(1)}, u32[]{:S(2)}, u32[]{:S(2)}) collective-permute-start(bf16[2,128,512]{2,1,0:T(8,128)(2,1)S(1)} %get-tuple-element.9), channel_id=1, source_target_pairs={{0,112},{16,0},{32,16},{48,32},{64,48},{80,64},{96,80},{112,96},{1... | collective-permute-start | bytes 786440 | tf_op jit(solution)/shard_map/ppermute | solution.py:45
  26.0 4.5 %collective-permute-done.2 = bf16[2,128,512]{2,1,0:T(8,128)(2,1)S(1)} collective-permute-done((bf16[2,128,512]{2,1,0:T(8,128)(2,1)S(1)}, bf16[2,128,512]{2,1,0:T(8,128)(2,1)S(1)}, u32[]{:S(2)}, u32[]{:S(2)}) %collective-permute-start.2) | collective-permute-done | bytes 262176 | tf_op jit(solution)/shard_map/ppermute | solution.py:44
  30.5 0.0 collective-permute-done.6
  30.5 1.4 %fusion.11 = (bf16[2,128,512]{2,1,0:T(8,128)(2,1)S(1)}, bf16[2,128,512]{2,1,0:T(8,128)(2,1)S(1)}) fusion(bf16[2,128,512]{2,1,0:T(8,128)(2,1)S(1)} %collective-permute-done.2, f32[2,8,128,512]{3,2,1,0:T(8,128)} %bitcast.141, s32[]{:T(128)S(6)} %select_n.147, bf16[2,8,128,512]{3,2,1,0:T(8,128)(2,1)S(1)} %bitcast.146, s32[]{:T(128)S(6)} %select_n.155, ...), kind=kLoop, calls=%fused_computation.23 | loop fusion | flops 1835008 | bytes 2621448 | tf_op jit(solution)/shard_map/convert_element_type | solution.py:56
  31.9 2.2 %collective-permute-start.3 = (bf16[2,128,512]{2,1,0:T(8,128)(2,1)S(1)}, bf16[2,128,512]{2,1,0:T(8,128)(2,1)S(1)}, u32[]{:S(2)}, u32[]{:S(2)}) collective-permute-start(bf16[2,128,512]{2,1,0:T(8,128)(2,1)S(1)} %get-tuple-element.6), channel_id=1, source_target_pairs={{0,16},{16,32},{32,48},{48,64},{64,80},{80,96},{96,112},{112,0},{1... | collective-permute-start | bytes 786440 | tf_op jit(solution)/shard_map/ppermute | solution.py:44
  34.1 1.1 %collective-permute-start.7 = (bf16[2,128,512]{2,1,0:T(8,128)(2,1)S(1)}, bf16[2,128,512]{2,1,0:T(8,128)(2,1)}, u32[]{:S(2)}, u32[]{:S(2)}) collective-permute-start(bf16[2,128,512]{2,1,0:T(8,128)(2,1)S(1)} %get-tuple-element.7), channel_id=1, source_target_pairs={{0,112},{16,0},{32,16},{48,32},{64,48},{80,64},{96,80},{112,96},{1... | collective-permute-start | bytes 786440 | tf_op jit(solution)/shard_map/ppermute | solution.py:45
  35.3 4.3 %collective-permute-done.3 = bf16[2,128,512]{2,1,0:T(8,128)(2,1)S(1)} collective-permute-done((bf16[2,128,512]{2,1,0:T(8,128)(2,1)S(1)}, bf16[2,128,512]{2,1,0:T(8,128)(2,1)S(1)}, u32[]{:S(2)}, u32[]{:S(2)}) %collective-permute-start.3) | collective-permute-done | bytes 262176 | tf_op jit(solution)/shard_map/ppermute | solution.py:44
  39.6 1.0 %collective-permute-done.7 = bf16[2,128,512]{2,1,0:T(8,128)(2,1)} collective-permute-done((bf16[2,128,512]{2,1,0:T(8,128)(2,1)S(1)}, bf16[2,128,512]{2,1,0:T(8,128)(2,1)}, u32[]{:S(2)}, u32[]{:S(2)}) %collective-permute-start.7) | collective-permute-done | bytes 262176 | tf_op jit(solution)/shard_map/ppermute | solution.py:45
  40.6 1.3 %fusion.14 = bf16[2,128,512]{2,1,0:T(8,128)(2,1)S(1)} fusion(bf16[2,128,512]{2,1,0:T(8,128)(2,1)} %collective-permute-done.7, bf16[2,128,512]{2,1,0:T(8,128)(2,1)S(1)} %collective-permute-done.3, f32[2,8,128,512]{3,2,1,0:T(8,128)} %bitcast.142, s32[]{:T(128)S(6)} %select_n.139, bf16[2,8,128,512]{3,2,1,0:T(8,128)(2,1)S(1)} %bitcast.147), kind=kLoop, calls=%fused_computation.28 | loop fusion | flops 1179648 | bytes 1572868 | tf_op jit(solution)/shard_map/convert_element_type | solution.py:58
  41.9 0.6 collective-permute-start.8
  42.5 3.0 %collective-permute-start.9 = (f32[128,512]{1,0:T(8,128)S(1)}, f32[128,512]{1,0:T(8,128)S(1)}, u32[]{:S(2)}, u32[]{:S(2)}) collective-permute-start(f32[128,512]{1,0:T(8,128)S(1)} %copy-done.2), channel_id=1, source_target_pairs={{0,128},{16,144},{32,160},{48,176},{64,192},{80,208},{96,224},{112... | collective-permute-start | bytes 786440 | tf_op jit(solution)/shard_map/ppermute | solution.py:103
  45.5 4.5 %collective-permute-done.8 = bf16[2,128,512]{2,1,0:T(8,128)(2,1)S(1)} collective-permute-done((bf16[2,128,512]{2,1,0:T(8,128)(2,1)S(1)}, bf16[2,128,512]{2,1,0:T(8,128)(2,1)S(1)}, u32[]{:S(2)}, u32[]{:S(2)}) %collective-permute-start.8) | collective-permute-done | bytes 262176 | tf_op jit(solution)/shard_map/ppermute | solution.py:59
  50.0 0.2 multiply_reduce_fusion
  50.1 0.6 broadcast_in_dim.38
  50.8 5.2 %all-to-all-start = ((f32[16,2,128]{2,1,0:T(2,128)}), f32[16,2,128]{2,1,0:T(2,128)S(1)}, u32[]{:S(2)}, u32[]{:S(2)}) async-start(f32[16,2,128]{2,1,0:T(2,128)} %broadcast_in_dim.38), calls=%async_computation | async-start | bytes 32768 | tf_op jit(solution)/shard_map/all_to_all | solution.py:111
  56.0 0.0 collective-permute-done.9
  56.0 6.0 %all-to-all-done = f32[16,2,128]{2,1,0:T(2,128)S(1)} async-done(((f32[16,2,128]{2,1,0:T(2,128)}), f32[16,2,128]{2,1,0:T(2,128)S(1)}, u32[]{:S(2)}, u32[]{:S(2)}) %all-to-all-start) | async-done | bytes 16416 | tf_op jit(solution)/shard_map/all_to_all | solution.py:111
  62.1 0.2 broadcast_in_dim.37
  62.3 1.3 %bitcast_dynamic-update-slice_fusion.6 = (bf16[2,8,128,512]{3,2,0,1:T(8,128)(2,1)S(1)}, bf16[2,128,512]{2,1,0:T(8,128)(2,1)S(1)}, f32[2,128,512]{2,1,0:T(8,128)S(1)}) fusion(bf16[2,8,128,512]{3,2,0,1:T(8,128)(2,1)S(1)} %broadcast_in_dim.37, s32[]{:T(128)S(6)} %select_n.139, f32[1,128,512]{2,1,0:T(8,128)S(1)} %get-tuple-element.15, ...), kind=kLoop, calls=%fused_computation.51 | loop fusion | flops 1572864 | bytes 2622472 | tf_op jit(solution)/shard_map/dynamic_update_slice | solution.py:70
  63.6 2.0 %collective-permute-start.10 = (bf16[2,128,512]{2,1,0:T(8,128)(2,1)S(1)}, bf16[2,128,512]{2,1,0:T(8,128)(2,1)S(1)}, u32[]{:S(2)}, u32[]{:S(2)}) collective-permute-start(bf16[2,128,512]{2,1,0:T(8,128)(2,1)S(1)} %get-tuple-element.4), channel_id=1, source_target_pairs={{0,16},{16,32},{32,48},{48,64},{64,80},{80,96},{96,112},{112,0},{1... | collective-permute-start | bytes 786440 | tf_op jit(solution)/shard_map/ppermute | solution.py:78
  65.6 1.3 %collective-permute-start.11 = (bf16[2,128,512]{2,1,0:T(8,128)(2,1)S(1)}, bf16[2,128,512]{2,1,0:T(8,128)(2,1)S(1)}, u32[]{:S(2)}, u32[]{:S(2)}) collective-permute-start(bf16[2,128,512]{2,1,0:T(8,128)(2,1)S(1)} %get-tuple-element.4), channel_id=1, source_target_pairs={{0,112},{16,0},{32,16},{48,32},{64,48},{80,64},{96,80},{112,96},{1... | collective-permute-start | bytes 786440 | tf_op jit(solution)/shard_map/ppermute | solution.py:79
  66.9 0.1 fusion
  67.0 0.7 dynamic-slice_bitcast_fusion
  67.8 0.7 dynamic-slice_bitcast_fusion.1
  68.5 4.7 %collective-permute-done.10 = bf16[2,128,512]{2,1,0:T(8,128)(2,1)S(1)} collective-permute-done((bf16[2,128,512]{2,1,0:T(8,128)(2,1)S(1)}, bf16[2,128,512]{2,1,0:T(8,128)(2,1)S(1)}, u32[]{:S(2)}, u32[]{:S(2)}) %collective-permute-start.10) | collective-permute-done | bytes 262176 | tf_op jit(solution)/shard_map/ppermute | solution.py:78
  73.2 0.7 collective-permute-start.12
  73.9 0.0 collective-permute-done.11
  73.9 2.5 %collective-permute-start.13 = (bf16[2,128,512]{2,1,0:T(8,128)(2,1)S(1)}, bf16[2,128,512]{2,1,0:T(8,128)(2,1)S(1)}, u32[]{:S(2)}, u32[]{:S(2)}) collective-permute-start(bf16[2,128,512]{2,1,0:T(8,128)(2,1)S(1)} %collective-permute-done.11), channel_id=1, source_target_pairs={{0,112},{16,0},{32,16},{48,32},{64,48},{80,64},{96,80},{112,96},{1... | collective-permute-start | bytes 786440 | tf_op jit(solution)/shard_map/ppermute | solution.py:79
  76.5 5.4 %collective-permute-done.12 = bf16[2,128,512]{2,1,0:T(8,128)(2,1)S(1)} collective-permute-done((bf16[2,128,512]{2,1,0:T(8,128)(2,1)S(1)}, bf16[2,128,512]{2,1,0:T(8,128)(2,1)S(1)}, u32[]{:S(2)}, u32[]{:S(2)}) %collective-permute-start.12) | collective-permute-done | bytes 262176 | tf_op jit(solution)/shard_map/ppermute | solution.py:78
  81.9 0.0 collective-permute-start.14
  81.9 3.2 %collective-permute-start.15 = (bf16[2,128,512]{2,1,0:T(8,128)(2,1)S(1)}, bf16[2,128,512]{2,1,0:T(8,128)(2,1)S(1)}, u32[]{:S(2)}, u32[]{:S(2)}) collective-permute-start(bf16[2,128,512]{2,1,0:T(8,128)(2,1)S(1)} %collective-permute-done.13), channel_id=1, source_target_pairs={{0,112},{16,0},{32,16},{48,32},{64,48},{80,64},{96,80},{112,96},{1... | collective-permute-start | bytes 786440 | tf_op jit(solution)/shard_map/ppermute | solution.py:79
  85.2 4.5 %collective-permute-done.14 = bf16[2,128,512]{2,1,0:T(8,128)(2,1)S(1)} collective-permute-done((bf16[2,128,512]{2,1,0:T(8,128)(2,1)S(1)}, bf16[2,128,512]{2,1,0:T(8,128)(2,1)S(1)}, u32[]{:S(2)}, u32[]{:S(2)}) %collective-permute-start.14) | collective-permute-done | bytes 262176 | tf_op jit(solution)/shard_map/ppermute | solution.py:78
  89.7 0.1 collective-permute-start.16
  89.8 3.3 %collective-permute-start.17 = (bf16[2,128,256]{2,1,0:T(8,128)(2,1)S(1)}, bf16[2,128,256]{2,1,0:T(8,128)(2,1)S(1)}, u32[]{:S(2)}, u32[]{:S(2)}) collective-permute-start(bf16[2,128,256]{2,1,0:T(8,128)(2,1)S(1)} %slice.49), channel_id=1, source_target_pairs={{0,112},{16,0},{32,16},{48,32},{64,48},{80,64},{96,80},{112,96},{1... | collective-permute-start | bytes 393224 | tf_op jit(solution)/shard_map/ppermute | solution.py:79
  93.2 2.8 %collective-permute-done.16 = bf16[2,128,256]{2,1,0:T(8,128)(2,1)S(1)} collective-permute-done((bf16[2,128,256]{2,1,0:T(8,128)(2,1)S(1)}, bf16[2,128,256]{2,1,0:T(8,128)(2,1)S(1)}, u32[]{:S(2)}, u32[]{:S(2)}) %collective-permute-start.16) | collective-permute-done | bytes 131104 | tf_op jit(solution)/shard_map/ppermute | solution.py:78
  96.0 0.2 copy.68
  96.2 0.0 copy-start.1
  96.2 1.3 %copy-done.1 = bf16[2,8,128,512]{3,2,1,0:T(8,128)(2,1)} copy-done((bf16[2,8,128,512]{3,2,1,0:T(8,128)(2,1)}, bf16[2,8,128,512]{3,2,1,0:T(8,128)(2,1)S(1)}, u32[]{:S(2)}) %copy-start.1) | copy-done | bytes 2097176
  (29 shorter events, 0.4 us)
Async XLA Ops:
  2.9 18.3 %copy-start = (bf16[1,2048,512]{2,1,0:T(8,128)(2,1)S(1)}, bf16[1,2048,512]{2,1,0:T(8,128)(2,1)}, u32[]{:S(2)}) copy-start(bf16[1,2048,512]{2,1,0:T(8,128)(2,1)} %param.4) | copy-start | bytes 6291460
  2.9 9.4 %collective-permute-start = (bf16[2,128,256]{2,1,0:T(8,128)(2,1)S(1)}, bf16[2,128,256]{2,1,0:T(8,128)(2,1)S(1)}, u32[]{:S(2)}, u32[]{:S(2)}) collective-permute-start(bf16[2,128,256]{2,1,0:T(8,128)(2,1)S(1)} %slice.42), channel_id=1, source_target_pairs={{0,16},{16,32},{32,48},{48,64},{64,80},{80,96},{96,112},{112,0},{1... | collective-permute-start | bytes 393224 | tf_op jit(solution)/shard_map/ppermute | solution.py:44
  5.0 7.6 %collective-permute-start.4 = (bf16[2,128,256]{2,1,0:T(8,128)(2,1)S(1)}, bf16[2,128,256]{2,1,0:T(8,128)(2,1)S(1)}, u32[]{:S(2)}, u32[]{:S(2)}) collective-permute-start(bf16[2,128,256]{2,1,0:T(8,128)(2,1)S(1)} %slice.46), channel_id=1, source_target_pairs={{0,112},{16,0},{32,16},{48,32},{64,48},{80,64},{96,80},{112,96},{1... | collective-permute-start | bytes 393224 | tf_op jit(solution)/shard_map/ppermute | solution.py:45
  12.4 8.8 %collective-permute-start.1 = (bf16[2,128,512]{2,1,0:T(8,128)(2,1)S(1)}, bf16[2,128,512]{2,1,0:T(8,128)(2,1)S(1)}, u32[]{:S(2)}, u32[]{:S(2)}) collective-permute-start(bf16[2,128,512]{2,1,0:T(8,128)(2,1)S(1)} %pad_maximum_fusion), channel_id=1, source_target_pairs={{0,16},{16,32},{32,48},{48,64},{64,80},{80,96},{96,112},{112,0},{1... | collective-permute-start | bytes 786440 | tf_op jit(solution)/shard_map/ppermute | solution.py:44
  12.6 8.6 %collective-permute-start.5 = (bf16[2,128,512]{2,1,0:T(8,128)(2,1)S(1)}, bf16[2,128,512]{2,1,0:T(8,128)(2,1)S(1)}, u32[]{:S(2)}, u32[]{:S(2)}) collective-permute-start(bf16[2,128,512]{2,1,0:T(8,128)(2,1)S(1)} %pad_maximum_fusion.1), channel_id=1, source_target_pairs={{0,112},{16,0},{32,16},{48,32},{64,48},{80,64},{96,80},{112,96},{1... | collective-permute-start | bytes 786440 | tf_op jit(solution)/shard_map/ppermute | solution.py:45
  22.7 7.9 %collective-permute-start.2 = (bf16[2,128,512]{2,1,0:T(8,128)(2,1)S(1)}, bf16[2,128,512]{2,1,0:T(8,128)(2,1)S(1)}, u32[]{:S(2)}, u32[]{:S(2)}) collective-permute-start(bf16[2,128,512]{2,1,0:T(8,128)(2,1)S(1)} %get-tuple-element.8), channel_id=1, source_target_pairs={{0,16},{16,32},{32,48},{48,64},{64,80},{80,96},{96,112},{112,0},{1... | collective-permute-start | bytes 786440 | tf_op jit(solution)/shard_map/ppermute | solution.py:44
  22.7 7.8 %collective-permute-start.6 = (bf16[2,128,512]{2,1,0:T(8,128)(2,1)S(1)}, bf16[2,128,512]{2,1,0:T(8,128)(2,1)S(1)}, u32[]{:S(2)}, u32[]{:S(2)}) collective-permute-start(bf16[2,128,512]{2,1,0:T(8,128)(2,1)S(1)} %get-tuple-element.9), channel_id=1, source_target_pairs={{0,112},{16,0},{32,16},{48,32},{64,48},{80,64},{96,80},{112,96},{1... | collective-permute-start | bytes 786440 | tf_op jit(solution)/shard_map/ppermute | solution.py:45
  26.0 16.5 %copy-start.2 = (f32[128,512]{1,0:T(8,128)S(1)}, f32[128,512]{1,0:T(8,128)}, u32[]{:S(2)}) copy-start(f32[128,512]{1,0:T(8,128)} %param.5) | copy-start | bytes 786436
  31.9 7.7 %collective-permute-start.3 = (bf16[2,128,512]{2,1,0:T(8,128)(2,1)S(1)}, bf16[2,128,512]{2,1,0:T(8,128)(2,1)S(1)}, u32[]{:S(2)}, u32[]{:S(2)}) collective-permute-start(bf16[2,128,512]{2,1,0:T(8,128)(2,1)S(1)} %get-tuple-element.6), channel_id=1, source_target_pairs={{0,16},{16,32},{32,48},{48,64},{64,80},{80,96},{96,112},{112,0},{1... | collective-permute-start | bytes 786440 | tf_op jit(solution)/shard_map/ppermute | solution.py:44
  34.1 6.5 %collective-permute-start.7 = (bf16[2,128,512]{2,1,0:T(8,128)(2,1)S(1)}, bf16[2,128,512]{2,1,0:T(8,128)(2,1)}, u32[]{:S(2)}, u32[]{:S(2)}) collective-permute-start(bf16[2,128,512]{2,1,0:T(8,128)(2,1)S(1)} %get-tuple-element.7), channel_id=1, source_target_pairs={{0,112},{16,0},{32,16},{48,32},{64,48},{80,64},{96,80},{112,96},{1... | collective-permute-start | bytes 786440 | tf_op jit(solution)/shard_map/ppermute | solution.py:45
  41.9 8.1 %collective-permute-start.8 = (bf16[2,128,512]{2,1,0:T(8,128)(2,1)S(1)}, bf16[2,128,512]{2,1,0:T(8,128)(2,1)S(1)}, u32[]{:S(2)}, u32[]{:S(2)}) collective-permute-start(bf16[2,128,512]{2,1,0:T(8,128)(2,1)S(1)} %fusion.14), channel_id=1, source_target_pairs={{0,128},{16,144},{32,160},{48,176},{64,192},{80,208},{96,224},{112... | collective-permute-start | bytes 786440 | tf_op jit(solution)/shard_map/ppermute | solution.py:59
  42.5 13.5 %collective-permute-start.9 = (f32[128,512]{1,0:T(8,128)S(1)}, f32[128,512]{1,0:T(8,128)S(1)}, u32[]{:S(2)}, u32[]{:S(2)}) collective-permute-start(f32[128,512]{1,0:T(8,128)S(1)} %copy-done.2), channel_id=1, source_target_pairs={{0,128},{16,144},{32,160},{48,176},{64,192},{80,208},{96,224},{112... | collective-permute-start | bytes 786440 | tf_op jit(solution)/shard_map/ppermute | solution.py:103
  50.8 11.3 %all-to-all-start = ((f32[16,2,128]{2,1,0:T(2,128)}), f32[16,2,128]{2,1,0:T(2,128)S(1)}, u32[]{:S(2)}, u32[]{:S(2)}) async-start(f32[16,2,128]{2,1,0:T(2,128)} %broadcast_in_dim.38), calls=%async_computation | async-start | bytes 32768 | tf_op jit(solution)/shard_map/all_to_all | solution.py:111
  63.6 9.6 %collective-permute-start.10 = (bf16[2,128,512]{2,1,0:T(8,128)(2,1)S(1)}, bf16[2,128,512]{2,1,0:T(8,128)(2,1)S(1)}, u32[]{:S(2)}, u32[]{:S(2)}) collective-permute-start(bf16[2,128,512]{2,1,0:T(8,128)(2,1)S(1)} %get-tuple-element.4), channel_id=1, source_target_pairs={{0,16},{16,32},{32,48},{48,64},{64,80},{80,96},{96,112},{112,0},{1... | collective-permute-start | bytes 786440 | tf_op jit(solution)/shard_map/ppermute | solution.py:78
  65.6 8.3 %collective-permute-start.11 = (bf16[2,128,512]{2,1,0:T(8,128)(2,1)S(1)}, bf16[2,128,512]{2,1,0:T(8,128)(2,1)S(1)}, u32[]{:S(2)}, u32[]{:S(2)}) collective-permute-start(bf16[2,128,512]{2,1,0:T(8,128)(2,1)S(1)} %get-tuple-element.4), channel_id=1, source_target_pairs={{0,112},{16,0},{32,16},{48,32},{64,48},{80,64},{96,80},{112,96},{1... | collective-permute-start | bytes 786440 | tf_op jit(solution)/shard_map/ppermute | solution.py:79
  73.2 8.7 %collective-permute-start.12 = (bf16[2,128,512]{2,1,0:T(8,128)(2,1)S(1)}, bf16[2,128,512]{2,1,0:T(8,128)(2,1)S(1)}, u32[]{:S(2)}, u32[]{:S(2)}) collective-permute-start(bf16[2,128,512]{2,1,0:T(8,128)(2,1)S(1)} %collective-permute-done.10), channel_id=1, source_target_pairs={{0,16},{16,32},{32,48},{48,64},{64,80},{80,96},{96,112},{112,0},{1... | collective-permute-start | bytes 786440 | tf_op jit(solution)/shard_map/ppermute | solution.py:78
  73.9 8.0 %collective-permute-start.13 = (bf16[2,128,512]{2,1,0:T(8,128)(2,1)S(1)}, bf16[2,128,512]{2,1,0:T(8,128)(2,1)S(1)}, u32[]{:S(2)}, u32[]{:S(2)}) collective-permute-start(bf16[2,128,512]{2,1,0:T(8,128)(2,1)S(1)} %collective-permute-done.11), channel_id=1, source_target_pairs={{0,112},{16,0},{32,16},{48,32},{64,48},{80,64},{96,80},{112,96},{1... | collective-permute-start | bytes 786440 | tf_op jit(solution)/shard_map/ppermute | solution.py:79
  81.9 7.8 %collective-permute-start.14 = (bf16[2,128,512]{2,1,0:T(8,128)(2,1)S(1)}, bf16[2,128,512]{2,1,0:T(8,128)(2,1)S(1)}, u32[]{:S(2)}, u32[]{:S(2)}) collective-permute-start(bf16[2,128,512]{2,1,0:T(8,128)(2,1)S(1)} %collective-permute-done.12), channel_id=1, source_target_pairs={{0,16},{16,32},{32,48},{48,64},{64,80},{80,96},{96,112},{112,0},{1... | collective-permute-start | bytes 786440 | tf_op jit(solution)/shard_map/ppermute | solution.py:78
  81.9 7.9 %collective-permute-start.15 = (bf16[2,128,512]{2,1,0:T(8,128)(2,1)S(1)}, bf16[2,128,512]{2,1,0:T(8,128)(2,1)S(1)}, u32[]{:S(2)}, u32[]{:S(2)}) collective-permute-start(bf16[2,128,512]{2,1,0:T(8,128)(2,1)S(1)} %collective-permute-done.13), channel_id=1, source_target_pairs={{0,112},{16,0},{32,16},{48,32},{64,48},{80,64},{96,80},{112,96},{1... | collective-permute-start | bytes 786440 | tf_op jit(solution)/shard_map/ppermute | solution.py:79
  89.7 6.3 %collective-permute-start.16 = (bf16[2,128,256]{2,1,0:T(8,128)(2,1)S(1)}, bf16[2,128,256]{2,1,0:T(8,128)(2,1)S(1)}, u32[]{:S(2)}, u32[]{:S(2)}) collective-permute-start(bf16[2,128,256]{2,1,0:T(8,128)(2,1)S(1)} %slice.48), channel_id=1, source_target_pairs={{0,16},{16,32},{32,48},{48,64},{64,80},{80,96},{96,112},{112,0},{1... | collective-permute-start | bytes 393224 | tf_op jit(solution)/shard_map/ppermute | solution.py:78
  89.8 6.3 %collective-permute-start.17 = (bf16[2,128,256]{2,1,0:T(8,128)(2,1)S(1)}, bf16[2,128,256]{2,1,0:T(8,128)(2,1)S(1)}, u32[]{:S(2)}, u32[]{:S(2)}) collective-permute-start(bf16[2,128,256]{2,1,0:T(8,128)(2,1)S(1)} %slice.49), channel_id=1, source_target_pairs={{0,112},{16,0},{32,16},{48,32},{64,48},{80,64},{96,80},{112,96},{1... | collective-permute-start | bytes 393224 | tf_op jit(solution)/shard_map/ppermute | solution.py:79
  96.2 1.3 %copy-start.1 = (bf16[2,8,128,512]{3,2,1,0:T(8,128)(2,1)}, bf16[2,8,128,512]{3,2,1,0:T(8,128)(2,1)S(1)}, u32[]{:S(2)}) copy-start(bf16[2,8,128,512]{3,2,1,0:T(8,128)(2,1)S(1)} %bitcast_dynamic-update-slice_fusion.7) | copy-start | bytes 6291460

commit v4 on v3

--- a/solution.py
+++ b/solution.py
@@ -38,15 +38,14 @@
     xh, z = r // nz, r % nz
     steps = nz // 2
     half = term(z).shape[-1] // 2
-    send_cw = term(z + steps)[..., :half]
-    send_ccw = term(z - steps)[..., half:]
+    send_cw, send_ccw = lax.optimization_barrier((term(z + steps)[..., :half], term(z - steps)[..., half:]))
     for s in range(steps):
         got_cw = lax.ppermute(send_cw, "rep", cw)
         got_ccw = lax.ppermute(send_ccw, "rep", ccw)
         if s == steps - 1:
             break
-        own_cw = f32(term(z + steps - 1 - s))
-        own_ccw = f32(term(z - steps + 1 + s))
+        own_cw, own_ccw = lax.optimization_barrier((term(z + steps - 1 - s), term(z - steps + 1 + s)))
+        own_cw, own_ccw = f32(own_cw), f32(own_ccw)
         if s == 0:
             send_cw = jnp.concatenate([f32(got_cw) + own_cw[..., :half], own_cw[..., half:]], axis=-1)
             send_ccw = jnp.concatenate([own_ccw[..., :half], f32(got_ccw) + own_ccw[..., half:]], axis=-1)
@@ -55,7 +54,8 @@
             send_ccw = f32(got_ccw) + own_ccw
         send_cw = send_cw.astype(jnp.bfloat16)
         send_ccw = send_ccw.astype(jnp.bfloat16)
-    total = (f32(term(z)) + f32(got_cw) + f32(got_ccw)).astype(jnp.bfloat16)
+    own = lax.optimization_barrier(term(z))
+    total = (f32(own) + f32(got_cw) + f32(got_ccw)).astype(jnp.bfloat16)
     return f32(total) + f32(lax.ppermute(total, "rep", xp))
 
 

time: 97.8 us -> 95.6 us (0.978)
  waiting for transfers between devices: 46.5 us -> 45.3 us
  other arithmetic: 8.07 us -> 6.88 us
    convert_element_type x2, other arithmetic: 2.84 us -> 0.13 us  [reduce_scatter(): send_cw = send_cw.astype(jnp.bfloat16)]
    ppermute x4, starting transfers between devices: 2.82 us -> 0.17 us  [all_gather(): cur_cw = lax.ppermute(cur_cw, 'rep', cw)]
    ppermute x4, starting transfers between devices: 10.3 us -> 13 us  [all_gather(): cur_ccw = lax.ppermute(cur_ccw, 'rep', ccw)]
    convert_element_type x1 -> x2, other arithmetic: 2.19 us -> 4.74 us  [term(): return (a - b.astype(jnp.float32)).astype(jnp.bfloat16)]
    ppermute x4, starting transfers between devices: 11.7 us -> 13.9 us  [reduce_scatter(): got_ccw = lax.ppermute(send_ccw, 'rep', ccw)]
    ppermute x4, starting transfers between devices: 4.34 us -> 2.25 us  [reduce_scatter(): got_cw = lax.ppermute(send_cw, 'rep', cw)]
    ppermute x4, waiting for transfers between devices: 17.6 us -> 16.1 us  [reduce_scatter(): got_cw = lax.ppermute(send_cw, 'rep', cw)]
    convert_element_type x1 -> x3, other arithmetic: 1.26 us -> 0.24 us  [the longest x2 0.14 us: reduce_scatter(): send_ccw = send_ccw.astype(jnp.bfloat16)]
  transfers between devices with their start and end apart: 19 -> 19, of which waited for: 11 -> 10; matrix products, arithmetic and copies ran while one was open for 3% -> 5% of each run, Pallas kernels for 0% -> 0%
where the time goes in v4:
time: 95.6 us; the launch traced here: 95.4 us
  waiting for transfers between devices  45.3 us (47%)
  starting transfers between devices  38.1 us (40%)
  other arithmetic  6.88 us (7%)
  local copies, waits for them, and re-layouts  3.99 us (4%)
  between operations  1.11 us (1%)
    ppermute x4, waiting for transfers between devices, all_gather(): cur_cw = lax.ppermute(cur_cw, 'rep', cw)  17.9 us
    ppermute x4, waiting for transfers between devices, reduce_scatter(): got_cw = lax.ppermute(send_cw, 'rep', cw)  16.1 us
    ppermute x4, starting transfers between devices, reduce_scatter(): got_ccw = lax.ppermute(send_ccw, 'rep', ccw)  13.9 us
    ppermute x4, starting transfers between devices, all_gather(): cur_ccw = lax.ppermute(cur_ccw, 'rep', ccw)  13 us
    all_to_all x1, waiting for transfers between devices, on_device(): lax.all_to_all(spread, 'fsdp', 0, 0, tiled=False)  6.02 us
    ppermute x1, waiting for transfers between devices, reduce_scatter(): return f32(total) + f32(lax.ppermute(total, 'rep', xp))  5.28 us
    all_to_all x1, starting transfers between devices, on_device(): lax.all_to_all(spread, 'fsdp', 0, 0, tiled=False)  5.21 us
    convert_element_type x2, other arithmetic, term(): return (a - b.astype(jnp.float32)).astype(jnp.bfloat16)  4.74 us
  transfers between devices with their start and end apart: 19, of which 10 were waited for; matrix products, arithmetic and copies ran while one was open for 5% of the time, Pallas kernels for 0%

profile of v4, /device:TPU:4, one launch (start us, length us, event | category | flops | bytes accessed | tf_op | source)
XLA Modules:
  0.0 95.4 jit_solution(1258180790901819012)
XLA Ops:
  0.8 3.6 %fusion.11 = (bf16[2,128,512]{2,1,0:T(8,128)(2,1)S(1)}, bf16[2,128,512]{2,1,0:T(8,128)(2,1)S(1)}, bf16[2,128,512]{2,1,0:T(8,128)(2,1)S(1)}, bf16[2,128,512]{2,1,...) fusion(f32[2,8,128,512]{3,2,1,0:T(8,128)} %bitcast.116, ...), kind=kLoop, calls=%fused_computation.29 | loop fusion | flops 3145728 | bytes 8388640 | tf_op jit(solution)/shard_map/convert_element_type | solution.py:99
  4.4 2.0 %collective-permute-start = (bf16[2,128,256]{2,1,0:T(8,128)(2,1)S(1)}, bf16[2,128,256]{2,1,0:T(8,128)(2,1)S(1)}, u32[]{:S(2)}, u32[]{:S(2)}) collective-permute-start(bf16[2,128,256]{2,1,0:T(8,128)(2,1)S(1)} %slice.42), channel_id=1, source_target_pairs={{0,16},{16,32},{32,48},{48,64},{64,80},{80,96},{96,112},{112,0},{1... | collective-permute-start | bytes 393224 | tf_op jit(solution)/shard_map/ppermute | solution.py:43
  6.4 4.0 %collective-permute-start.4 = (bf16[2,128,256]{2,1,0:T(8,128)(2,1)S(1)}, bf16[2,128,256]{2,1,0:T(8,128)(2,1)S(1)}, u32[]{:S(2)}, u32[]{:S(2)}) collective-permute-start(bf16[2,128,256]{2,1,0:T(8,128)(2,1)S(1)} %slice.43), channel_id=1, source_target_pairs={{0,112},{16,0},{32,16},{48,32},{64,48},{80,64},{96,80},{112,96},{1... | collective-permute-start | bytes 393224 | tf_op jit(solution)/shard_map/ppermute | solution.py:44
  10.5 3.4 %collective-permute-done = bf16[2,128,256]{2,1,0:T(8,128)(2,1)S(1)} collective-permute-done((bf16[2,128,256]{2,1,0:T(8,128)(2,1)S(1)}, bf16[2,128,256]{2,1,0:T(8,128)(2,1)S(1)}, u32[]{:S(2)}, u32[]{:S(2)}) %collective-permute-start) | collective-permute-done | bytes 131104 | tf_op jit(solution)/shard_map/ppermute | solution.py:43
  13.9 0.1 collective-permute-start.1
  14.1 3.3 %collective-permute-start.5 = (bf16[2,128,512]{2,1,0:T(8,128)(2,1)S(1)}, bf16[2,128,512]{2,1,0:T(8,128)(2,1)S(1)}, u32[]{:S(2)}, u32[]{:S(2)}) collective-permute-start(bf16[2,128,512]{2,1,0:T(8,128)(2,1)S(1)} %pad_maximum_fusion.1), channel_id=1, source_target_pairs={{0,112},{16,0},{32,16},{48,32},{64,48},{80,64},{96,80},{112,96},{1... | collective-permute-start | bytes 786440 | tf_op jit(solution)/shard_map/ppermute | solution.py:44
  17.4 5.3 %collective-permute-done.1 = bf16[2,128,512]{2,1,0:T(8,128)(2,1)S(1)} collective-permute-done((bf16[2,128,512]{2,1,0:T(8,128)(2,1)S(1)}, bf16[2,128,512]{2,1,0:T(8,128)(2,1)S(1)}, u32[]{:S(2)}, u32[]{:S(2)}) %collective-permute-start.1) | collective-permute-done | bytes 262176 | tf_op jit(solution)/shard_map/ppermute | solution.py:43
  22.7 0.1 add_convert_fusion.4
  22.8 0.0 copy-start.1
  22.8 0.1 collective-permute-start.2
  22.9 0.0 collective-permute-done.5
  22.9 0.1 add_convert_fusion.2
  22.9 3.3 %collective-permute-start.6 = (bf16[2,128,512]{2,1,0:T(8,128)(2,1)S(1)}, bf16[2,128,512]{2,1,0:T(8,128)(2,1)S(1)}, u32[]{:S(2)}, u32[]{:S(2)}) collective-permute-start(bf16[2,128,512]{2,1,0:T(8,128)(2,1)S(1)} %add_convert_fusion.2), channel_id=1, source_target_pairs={{0,112},{16,0},{32,16},{48,32},{64,48},{80,64},{96,80},{112,96},{1... | collective-permute-start | bytes 786440 | tf_op jit(solution)/shard_map/ppermute | solution.py:44
  26.2 1.2 %fusion.10 = bf16[2,128,512]{2,1,0:T(8,128)(2,1)S(1)} fusion(f32[2,8,128,512]{3,2,1,0:T(8,128)} %bitcast.117, s32[]{:T(128)S(6)} %select_n.155, bf16[2,8,128,512]{3,2,1,0:T(8,128)(2,1)} %bitcast.120), kind=kLoop, calls=%fused_computation.28 | loop fusion | flops 393216 | bytes 1048580 | tf_op jit(solution)/shard_map/convert_element_type | solution.py:99
  27.4 3.2 %collective-permute-done.2 = bf16[2,128,512]{2,1,0:T(8,128)(2,1)S(1)} collective-permute-done((bf16[2,128,512]{2,1,0:T(8,128)(2,1)S(1)}, bf16[2,128,512]{2,1,0:T(8,128)(2,1)S(1)}, u32[]{:S(2)}, u32[]{:S(2)}) %collective-permute-start.2) | collective-permute-done | bytes 262176 | tf_op jit(solution)/shard_map/ppermute | solution.py:43
  30.6 0.1 add_convert_fusion.3
  30.7 0.1 collective-permute-start.3
  30.8 0.1 add_convert_fusion.1
  30.9 3.3 %collective-permute-start.7 = (bf16[2,128,512]{2,1,0:T(8,128)(2,1)S(1)}, bf16[2,128,512]{2,1,0:T(8,128)(2,1)S(1)}, u32[]{:S(2)}, u32[]{:S(2)}) collective-permute-start(bf16[2,128,512]{2,1,0:T(8,128)(2,1)S(1)} %add_convert_fusion.1), channel_id=1, source_target_pairs={{0,112},{16,0},{32,16},{48,32},{64,48},{80,64},{96,80},{112,96},{1... | collective-permute-start | bytes 786440 | tf_op jit(solution)/shard_map/ppermute | solution.py:44
  34.2 4.2 %collective-permute-done.3 = bf16[2,128,512]{2,1,0:T(8,128)(2,1)S(1)} collective-permute-done((bf16[2,128,512]{2,1,0:T(8,128)(2,1)S(1)}, bf16[2,128,512]{2,1,0:T(8,128)(2,1)S(1)}, u32[]{:S(2)}, u32[]{:S(2)}) %collective-permute-start.3) | collective-permute-done | bytes 262176 | tf_op jit(solution)/shard_map/ppermute | solution.py:43
  38.4 0.0 collective-permute-done.7
  38.4 0.1 add_convert_fusion
  38.5 0.6 collective-permute-start.8
  39.1 3.0 %collective-permute-start.9 = (f32[128,512]{1,0:T(8,128)S(1)}, f32[128,512]{1,0:T(8,128)S(1)}, u32[]{:S(2)}, u32[]{:S(2)}) collective-permute-start(f32[128,512]{1,0:T(8,128)S(1)} %copy-done.1), channel_id=1, source_target_pairs={{0,128},{16,144},{32,160},{48,176},{64,192},{80,208},{96,224},{112... | collective-permute-start | bytes 786440 | tf_op jit(solution)/shard_map/ppermute | solution.py:103
  42.1 5.3 %collective-permute-done.8 = bf16[2,128,512]{2,1,0:T(8,128)(2,1)S(1)} collective-permute-done((bf16[2,128,512]{2,1,0:T(8,128)(2,1)S(1)}, bf16[2,128,512]{2,1,0:T(8,128)(2,1)S(1)}, u32[]{:S(2)}, u32[]{:S(2)}) %collective-permute-start.8) | collective-permute-done | bytes 262176 | tf_op jit(solution)/shard_map/ppermute | solution.py:59
  47.4 0.2 multiply_reduce_fusion
  47.5 0.6 broadcast_in_dim.38
  48.2 5.2 %all-to-all-start = ((f32[16,2,128]{2,1,0:T(2,128)}), f32[16,2,128]{2,1,0:T(2,128)S(1)}, u32[]{:S(2)}, u32[]{:S(2)}) async-start(f32[16,2,128]{2,1,0:T(2,128)} %broadcast_in_dim.38), calls=%async_computation | async-start | bytes 32768 | tf_op jit(solution)/shard_map/all_to_all | solution.py:111
  53.4 6.0 %all-to-all-done = f32[16,2,128]{2,1,0:T(2,128)S(1)} async-done(((f32[16,2,128]{2,1,0:T(2,128)}), f32[16,2,128]{2,1,0:T(2,128)S(1)}, u32[]{:S(2)}, u32[]{:S(2)}) %all-to-all-start) | async-done | bytes 16416 | tf_op jit(solution)/shard_map/all_to_all | solution.py:111
  59.5 0.2 broadcast_in_dim.37
  59.7 1.3 %bitcast_dynamic-update-slice_fusion.6 = (bf16[2,8,128,512]{3,2,0,1:T(8,128)(2,1)S(1)}, bf16[2,128,512]{2,1,0:T(8,128)(2,1)S(1)}, f32[2,128,512]{2,1,0:T(8,128)S(1)}) fusion(bf16[2,8,128,512]{3,2,0,1:T(8,128)(2,1)S(1)} %broadcast_in_dim.37, s32[]{:T(128)S(6)} %select_n.139, f32[1,128,512]{2,1,0:T(8,128)S(1)} %get-tuple-element.31, ...), kind=kLoop, calls=%fused_computation.45 | loop fusion | flops 1572864 | bytes 2622472 | tf_op jit(solution)/shard_map/dynamic_update_slice | solution.py:70
  61.0 0.1 collective-permute-start.10
  61.1 3.2 %collective-permute-start.11 = (bf16[2,128,512]{2,1,0:T(8,128)(2,1)S(1)}, bf16[2,128,512]{2,1,0:T(8,128)(2,1)S(1)}, u32[]{:S(2)}, u32[]{:S(2)}) collective-permute-start(bf16[2,128,512]{2,1,0:T(8,128)(2,1)S(1)} %get-tuple-element.20), channel_id=1, source_target_pairs={{0,112},{16,0},{32,16},{48,32},{64,48},{80,64},{96,80},{112,96},{1... | collective-permute-start | bytes 786440 | tf_op jit(solution)/shard_map/ppermute | solution.py:79
  64.3 0.1 fusion
  64.4 0.7 dynamic-slice_bitcast_fusion
  65.2 0.7 dynamic-slice_bitcast_fusion.1
  65.9 4.9 %collective-permute-done.10 = bf16[2,128,512]{2,1,0:T(8,128)(2,1)S(1)} collective-permute-done((bf16[2,128,512]{2,1,0:T(8,128)(2,1)S(1)}, bf16[2,128,512]{2,1,0:T(8,128)(2,1)S(1)}, u32[]{:S(2)}, u32[]{:S(2)}) %collective-permute-start.10) | collective-permute-done | bytes 262176 | tf_op jit(solution)/shard_map/ppermute | solution.py:78
  70.7 0.0 collective-permute-start.12
  70.8 3.2 %collective-permute-start.13 = (bf16[2,128,512]{2,1,0:T(8,128)(2,1)S(1)}, bf16[2,128,512]{2,1,0:T(8,128)(2,1)S(1)}, u32[]{:S(2)}, u32[]{:S(2)}) collective-permute-start(bf16[2,128,512]{2,1,0:T(8,128)(2,1)S(1)} %collective-permute-done.11), channel_id=1, source_target_pairs={{0,112},{16,0},{32,16},{48,32},{64,48},{80,64},{96,80},{112,96},{1... | collective-permute-start | bytes 786440 | tf_op jit(solution)/shard_map/ppermute | solution.py:79
  74.0 5.6 %collective-permute-done.12 = bf16[2,128,512]{2,1,0:T(8,128)(2,1)S(1)} collective-permute-done((bf16[2,128,512]{2,1,0:T(8,128)(2,1)S(1)}, bf16[2,128,512]{2,1,0:T(8,128)(2,1)S(1)}, u32[]{:S(2)}, u32[]{:S(2)}) %collective-permute-start.12) | collective-permute-done | bytes 262176 | tf_op jit(solution)/shard_map/ppermute | solution.py:78
  79.6 3.2 %collective-permute-start.15 = (bf16[2,128,512]{2,1,0:T(8,128)(2,1)S(1)}, bf16[2,128,512]{2,1,0:T(8,128)(2,1)S(1)}, u32[]{:S(2)}, u32[]{:S(2)}) collective-permute-start(bf16[2,128,512]{2,1,0:T(8,128)(2,1)S(1)} %collective-permute-done.13), channel_id=1, source_target_pairs={{0,112},{16,0},{32,16},{48,32},{64,48},{80,64},{96,80},{112,96},{1... | collective-permute-start | bytes 786440 | tf_op jit(solution)/shard_map/ppermute | solution.py:79
  82.9 4.7 %collective-permute-done.14 = bf16[2,128,512]{2,1,0:T(8,128)(2,1)S(1)} collective-permute-done((bf16[2,128,512]{2,1,0:T(8,128)(2,1)S(1)}, bf16[2,128,512]{2,1,0:T(8,128)(2,1)S(1)}, u32[]{:S(2)}, u32[]{:S(2)}) %collective-permute-start.14) | collective-permute-done | bytes 262176 | tf_op jit(solution)/shard_map/ppermute | solution.py:78
  87.6 0.1 collective-permute-start.16
  87.7 3.3 %collective-permute-start.17 = (bf16[2,128,256]{2,1,0:T(8,128)(2,1)S(1)}, bf16[2,128,256]{2,1,0:T(8,128)(2,1)S(1)}, u32[]{:S(2)}, u32[]{:S(2)}) collective-permute-start(bf16[2,128,256]{2,1,0:T(8,128)(2,1)S(1)} %slice.45), channel_id=1, source_target_pairs={{0,112},{16,0},{32,16},{48,32},{64,48},{80,64},{96,80},{112,96},{1... | collective-permute-start | bytes 393224 | tf_op jit(solution)/shard_map/ppermute | solution.py:79
  91.1 2.8 %collective-permute-done.16 = bf16[2,128,256]{2,1,0:T(8,128)(2,1)S(1)} collective-permute-done((bf16[2,128,256]{2,1,0:T(8,128)(2,1)S(1)}, bf16[2,128,256]{2,1,0:T(8,128)(2,1)S(1)}, u32[]{:S(2)}, u32[]{:S(2)}) %collective-permute-start.16) | collective-permute-done | bytes 131104 | tf_op jit(solution)/shard_map/ppermute | solution.py:78
  93.9 0.2 copy.68
  94.1 0.0 copy-start
  94.1 1.3 %copy-done = bf16[2,8,128,512]{3,2,1,0:T(8,128)(2,1)} copy-done((bf16[2,8,128,512]{3,2,1,0:T(8,128)(2,1)}, bf16[2,8,128,512]{3,2,1,0:T(8,128)(2,1)S(1)}, u32[]{:S(2)}) %copy-start) | copy-done | bytes 2097176
  (30 shorter events, 0.4 us)
Async XLA Ops:
  4.4 9.4 %collective-permute-start = (bf16[2,128,256]{2,1,0:T(8,128)(2,1)S(1)}, bf16[2,128,256]{2,1,0:T(8,128)(2,1)S(1)}, u32[]{:S(2)}, u32[]{:S(2)}) collective-permute-start(bf16[2,128,256]{2,1,0:T(8,128)(2,1)S(1)} %slice.42), channel_id=1, source_target_pairs={{0,16},{16,32},{32,48},{48,64},{64,80},{80,96},{96,112},{112,0},{1... | collective-permute-start | bytes 393224 | tf_op jit(solution)/shard_map/ppermute | solution.py:43
  6.4 7.6 %collective-permute-start.4 = (bf16[2,128,256]{2,1,0:T(8,128)(2,1)S(1)}, bf16[2,128,256]{2,1,0:T(8,128)(2,1)S(1)}, u32[]{:S(2)}, u32[]{:S(2)}) collective-permute-start(bf16[2,128,256]{2,1,0:T(8,128)(2,1)S(1)} %slice.43), channel_id=1, source_target_pairs={{0,112},{16,0},{32,16},{48,32},{64,48},{80,64},{96,80},{112,96},{1... | collective-permute-start | bytes 393224 | tf_op jit(solution)/shard_map/ppermute | solution.py:44
  13.9 8.8 %collective-permute-start.1 = (bf16[2,128,512]{2,1,0:T(8,128)(2,1)S(1)}, bf16[2,128,512]{2,1,0:T(8,128)(2,1)S(1)}, u32[]{:S(2)}, u32[]{:S(2)}) collective-permute-start(bf16[2,128,512]{2,1,0:T(8,128)(2,1)S(1)} %pad_maximum_fusion), channel_id=1, source_target_pairs={{0,16},{16,32},{32,48},{48,64},{64,80},{80,96},{96,112},{112,0},{1... | collective-permute-start | bytes 786440 | tf_op jit(solution)/shard_map/ppermute | solution.py:43
  14.1 8.8 %collective-permute-start.5 = (bf16[2,128,512]{2,1,0:T(8,128)(2,1)S(1)}, bf16[2,128,512]{2,1,0:T(8,128)(2,1)S(1)}, u32[]{:S(2)}, u32[]{:S(2)}) collective-permute-start(bf16[2,128,512]{2,1,0:T(8,128)(2,1)S(1)} %pad_maximum_fusion.1), channel_id=1, source_target_pairs={{0,112},{16,0},{32,16},{48,32},{64,48},{80,64},{96,80},{112,96},{1... | collective-permute-start | bytes 786440 | tf_op jit(solution)/shard_map/ppermute | solution.py:44
  22.8 16.3 %copy-start.1 = (f32[128,512]{1,0:T(8,128)S(1)}, f32[128,512]{1,0:T(8,128)}, u32[]{:S(2)}) copy-start(f32[128,512]{1,0:T(8,128)} %param.5) | copy-start | bytes 786436
  22.8 7.9 %collective-permute-start.2 = (bf16[2,128,512]{2,1,0:T(8,128)(2,1)S(1)}, bf16[2,128,512]{2,1,0:T(8,128)(2,1)S(1)}, u32[]{:S(2)}, u32[]{:S(2)}) collective-permute-start(bf16[2,128,512]{2,1,0:T(8,128)(2,1)S(1)} %add_convert_fusion.4), channel_id=1, source_target_pairs={{0,16},{16,32},{32,48},{48,64},{64,80},{80,96},{96,112},{112,0},{1... | collective-permute-start | bytes 786440 | tf_op jit(solution)/shard_map/ppermute | solution.py:43
  22.9 7.8 %collective-permute-start.6 = (bf16[2,128,512]{2,1,0:T(8,128)(2,1)S(1)}, bf16[2,128,512]{2,1,0:T(8,128)(2,1)S(1)}, u32[]{:S(2)}, u32[]{:S(2)}) collective-permute-start(bf16[2,128,512]{2,1,0:T(8,128)(2,1)S(1)} %add_convert_fusion.2), channel_id=1, source_target_pairs={{0,112},{16,0},{32,16},{48,32},{64,48},{80,64},{96,80},{112,96},{1... | collective-permute-start | bytes 786440 | tf_op jit(solution)/shard_map/ppermute | solution.py:44
  30.7 7.7 %collective-permute-start.3 = (bf16[2,128,512]{2,1,0:T(8,128)(2,1)S(1)}, bf16[2,128,512]{2,1,0:T(8,128)(2,1)S(1)}, u32[]{:S(2)}, u32[]{:S(2)}) collective-permute-start(bf16[2,128,512]{2,1,0:T(8,128)(2,1)S(1)} %add_convert_fusion.3), channel_id=1, source_target_pairs={{0,16},{16,32},{32,48},{48,64},{64,80},{80,96},{96,112},{112,0},{1... | collective-permute-start | bytes 786440 | tf_op jit(solution)/shard_map/ppermute | solution.py:43
  30.9 7.5 %collective-permute-start.7 = (bf16[2,128,512]{2,1,0:T(8,128)(2,1)S(1)}, bf16[2,128,512]{2,1,0:T(8,128)(2,1)S(1)}, u32[]{:S(2)}, u32[]{:S(2)}) collective-permute-start(bf16[2,128,512]{2,1,0:T(8,128)(2,1)S(1)} %add_convert_fusion.1), channel_id=1, source_target_pairs={{0,112},{16,0},{32,16},{48,32},{64,48},{80,64},{96,80},{112,96},{1... | collective-permute-start | bytes 786440 | tf_op jit(solution)/shard_map/ppermute | solution.py:44
  38.5 8.9 %collective-permute-start.8 = (bf16[2,128,512]{2,1,0:T(8,128)(2,1)S(1)}, bf16[2,128,512]{2,1,0:T(8,128)(2,1)S(1)}, u32[]{:S(2)}, u32[]{:S(2)}) collective-permute-start(bf16[2,128,512]{2,1,0:T(8,128)(2,1)S(1)} %add_convert_fusion), channel_id=1, source_target_pairs={{0,128},{16,144},{32,160},{48,176},{64,192},{80,208},{96,224},{112... | collective-permute-start | bytes 786440 | tf_op jit(solution)/shard_map/ppermute | solution.py:59
  39.1 14.3 %collective-permute-start.9 = (f32[128,512]{1,0:T(8,128)S(1)}, f32[128,512]{1,0:T(8,128)S(1)}, u32[]{:S(2)}, u32[]{:S(2)}) collective-permute-start(f32[128,512]{1,0:T(8,128)S(1)} %copy-done.1), channel_id=1, source_target_pairs={{0,128},{16,144},{32,160},{48,176},{64,192},{80,208},{96,224},{112... | collective-permute-start | bytes 786440 | tf_op jit(solution)/shard_map/ppermute | solution.py:103
  48.2 11.3 %all-to-all-start = ((f32[16,2,128]{2,1,0:T(2,128)}), f32[16,2,128]{2,1,0:T(2,128)S(1)}, u32[]{:S(2)}, u32[]{:S(2)}) async-start(f32[16,2,128]{2,1,0:T(2,128)} %broadcast_in_dim.38), calls=%async_computation | async-start | bytes 32768 | tf_op jit(solution)/shard_map/all_to_all | solution.py:111
  61.0 9.8 %collective-permute-start.10 = (bf16[2,128,512]{2,1,0:T(8,128)(2,1)S(1)}, bf16[2,128,512]{2,1,0:T(8,128)(2,1)S(1)}, u32[]{:S(2)}, u32[]{:S(2)}) collective-permute-start(bf16[2,128,512]{2,1,0:T(8,128)(2,1)S(1)} %get-tuple-element.20), channel_id=1, source_target_pairs={{0,16},{16,32},{32,48},{48,64},{64,80},{80,96},{96,112},{112,0},{1... | collective-permute-start | bytes 786440 | tf_op jit(solution)/shard_map/ppermute | solution.py:78
  61.1 9.7 %collective-permute-start.11 = (bf16[2,128,512]{2,1,0:T(8,128)(2,1)S(1)}, bf16[2,128,512]{2,1,0:T(8,128)(2,1)S(1)}, u32[]{:S(2)}, u32[]{:S(2)}) collective-permute-start(bf16[2,128,512]{2,1,0:T(8,128)(2,1)S(1)} %get-tuple-element.20), channel_id=1, source_target_pairs={{0,112},{16,0},{32,16},{48,32},{64,48},{80,64},{96,80},{112,96},{1... | collective-permute-start | bytes 786440 | tf_op jit(solution)/shard_map/ppermute | solution.py:79
  70.7 8.9 %collective-permute-start.12 = (bf16[2,128,512]{2,1,0:T(8,128)(2,1)S(1)}, bf16[2,128,512]{2,1,0:T(8,128)(2,1)S(1)}, u32[]{:S(2)}, u32[]{:S(2)}) collective-permute-start(bf16[2,128,512]{2,1,0:T(8,128)(2,1)S(1)} %collective-permute-done.10), channel_id=1, source_target_pairs={{0,16},{16,32},{32,48},{48,64},{64,80},{80,96},{96,112},{112,0},{1... | collective-permute-start | bytes 786440 | tf_op jit(solution)/shard_map/ppermute | solution.py:78
  70.8 8.9 %collective-permute-start.13 = (bf16[2,128,512]{2,1,0:T(8,128)(2,1)S(1)}, bf16[2,128,512]{2,1,0:T(8,128)(2,1)S(1)}, u32[]{:S(2)}, u32[]{:S(2)}) collective-permute-start(bf16[2,128,512]{2,1,0:T(8,128)(2,1)S(1)} %collective-permute-done.11), channel_id=1, source_target_pairs={{0,112},{16,0},{32,16},{48,32},{64,48},{80,64},{96,80},{112,96},{1... | collective-permute-start | bytes 786440 | tf_op jit(solution)/shard_map/ppermute | solution.py:79
  79.6 8.0 %collective-permute-start.14 = (bf16[2,128,512]{2,1,0:T(8,128)(2,1)S(1)}, bf16[2,128,512]{2,1,0:T(8,128)(2,1)S(1)}, u32[]{:S(2)}, u32[]{:S(2)}) collective-permute-start(bf16[2,128,512]{2,1,0:T(8,128)(2,1)S(1)} %collective-permute-done.12), channel_id=1, source_target_pairs={{0,16},{16,32},{32,48},{48,64},{64,80},{80,96},{96,112},{112,0},{1... | collective-permute-start | bytes 786440 | tf_op jit(solution)/shard_map/ppermute | solution.py:78
  79.6 8.1 %collective-permute-start.15 = (bf16[2,128,512]{2,1,0:T(8,128)(2,1)S(1)}, bf16[2,128,512]{2,1,0:T(8,128)(2,1)S(1)}, u32[]{:S(2)}, u32[]{:S(2)}) collective-permute-start(bf16[2,128,512]{2,1,0:T(8,128)(2,1)S(1)} %collective-permute-done.13), channel_id=1, source_target_pairs={{0,112},{16,0},{32,16},{48,32},{64,48},{80,64},{96,80},{112,96},{1... | collective-permute-start | bytes 786440 | tf_op jit(solution)/shard_map/ppermute | solution.py:79
  87.6 6.3 %collective-permute-start.16 = (bf16[2,128,256]{2,1,0:T(8,128)(2,1)S(1)}, bf16[2,128,256]{2,1,0:T(8,128)(2,1)S(1)}, u32[]{:S(2)}, u32[]{:S(2)}) collective-permute-start(bf16[2,128,256]{2,1,0:T(8,128)(2,1)S(1)} %slice.44), channel_id=1, source_target_pairs={{0,16},{16,32},{32,48},{48,64},{64,80},{80,96},{96,112},{112,0},{1... | collective-permute-start | bytes 393224 | tf_op jit(solution)/shard_map/ppermute | solution.py:78
  87.7 6.3 %collective-permute-start.17 = (bf16[2,128,256]{2,1,0:T(8,128)(2,1)S(1)}, bf16[2,128,256]{2,1,0:T(8,128)(2,1)S(1)}, u32[]{:S(2)}, u32[]{:S(2)}) collective-permute-start(bf16[2,128,256]{2,1,0:T(8,128)(2,1)S(1)} %slice.45), channel_id=1, source_target_pairs={{0,112},{16,0},{32,16},{48,32},{64,48},{80,64},{96,80},{112,96},{1... | collective-permute-start | bytes 393224 | tf_op jit(solution)/shard_map/ppermute | solution.py:79
  94.1 1.3 %copy-start = (bf16[2,8,128,512]{3,2,1,0:T(8,128)(2,1)}, bf16[2,8,128,512]{3,2,1,0:T(8,128)(2,1)S(1)}, u32[]{:S(2)}) copy-start(bf16[2,8,128,512]{3,2,1,0:T(8,128)(2,1)S(1)} %bitcast_dynamic-update-slice_fusion.7) | copy-start | bytes 6291460

commit v5 on v4

--- a/solution.py
+++ b/solution.py
@@ -37,8 +37,7 @@
     r = lax.axis_index("rep")
     xh, z = r // nz, r % nz
     steps = nz // 2
-    half = term(z).shape[-1] // 2
-    send_cw, send_ccw = lax.optimization_barrier((term(z + steps)[..., :half], term(z - steps)[..., half:]))
+    send_cw, send_ccw = lax.optimization_barrier((term(z + steps)[:1], term(z - steps)[1:]))
     for s in range(steps):
         got_cw = lax.ppermute(send_cw, "rep", cw)
         got_ccw = lax.ppermute(send_ccw, "rep", ccw)
@@ -47,8 +46,8 @@
         own_cw, own_ccw = lax.optimization_barrier((term(z + steps - 1 - s), term(z - steps + 1 + s)))
         own_cw, own_ccw = f32(own_cw), f32(own_ccw)
         if s == 0:
-            send_cw = jnp.concatenate([f32(got_cw) + own_cw[..., :half], own_cw[..., half:]], axis=-1)
-            send_ccw = jnp.concatenate([own_ccw[..., :half], f32(got_ccw) + own_ccw[..., half:]], axis=-1)
+            send_cw = jnp.concatenate([f32(got_cw) + own_cw[:1], own_cw[1:]])
+            send_ccw = jnp.concatenate([own_ccw[:1], f32(got_ccw) + own_ccw[1:]])
         else:
             send_cw = f32(got_cw) + own_cw
             send_ccw = f32(got_ccw) + own_ccw
@@ -65,20 +64,19 @@
     xh, z = r // nz, r % nz
     blk = w
     rows, cols = w.shape[1:]
-    half = cols // 2
     out = jnp.zeros((NX, nz, rows, cols), w.dtype)
-    put = lambda o, piece, pos, col: lax.dynamic_update_slice(o, piece[:, None], (0, pos % nz, 0, col))
+    put = lambda o, piece, pos, row: lax.dynamic_update_slice(o, piece[:, None], (row, pos % nz, 0, 0))
     out = put(out, blk, z, 0)
     steps = nz // 2
     cur_cw, cur_ccw = blk, blk
     for s in range(steps):
         if s == steps - 1:
-            cur_cw = cur_cw[..., :half]
-            cur_ccw = cur_ccw[..., half:]
+            cur_cw = cur_cw[:1]
+            cur_ccw = cur_ccw[1:]
         cur_cw = lax.ppermute(cur_cw, "rep", cw)
         cur_ccw = lax.ppermute(cur_ccw, "rep", ccw)
         out = put(out, cur_cw, z - 1 - s, 0)
-        out = put(out, cur_ccw, z + 1 + s, half if s == steps - 1 else 0)
+        out = put(out, cur_ccw, z + 1 + s, 1 if s == steps - 1 else 0)
     return out.reshape(n * rows, cols)
 
 

time: 95.6 us -> 94.3 us (0.986)
  waiting for transfers between devices: 45.3 us -> 42.5 us
  starting transfers between devices: 38.1 us -> 39.4 us
    ppermute x4, waiting for transfers between devices: 16.1 us -> 3.86 us  [reduce_scatter(): got_cw = lax.ppermute(send_cw, 'rep', cw)]
    ppermute x4, waiting for transfers between devices: 0.01 us -> 10.8 us  [reduce_scatter(): got_ccw = lax.ppermute(send_ccw, 'rep', ccw)]
    ppermute x4, starting transfers between devices: 13.9 us -> 15.2 us  [reduce_scatter(): got_ccw = lax.ppermute(send_ccw, 'rep', ccw)]
    slice x0 -> x1, other arithmetic: none -> 1.18 us  [reduce_scatter(): term(z - steps)[1:]]
  transfers between devices with their start and end apart: 19 -> 19, of which waited for: 10 -> 10; matrix products, arithmetic and copies ran while one was open for 5% -> 7% of each run, Pallas kernels for 0% -> 0%
where the time goes in v5:
time: 94.3 us; the launch traced here: 94 us
  waiting for transfers between devices  42.5 us (45%)
  starting transfers between devices  39.4 us (42%)
  other arithmetic  7.35 us (8%)
  local copies, waits for them, and re-layouts  3.79 us (4%)
  between operations  0.99 us (1%)
    ppermute x4, waiting for transfers between devices, all_gather(): cur_cw = lax.ppermute(cur_cw, 'rep', cw)  17.4 us
    ppermute x4, starting transfers between devices, reduce_scatter(): got_ccw = lax.ppermute(send_ccw, 'rep', ccw)  15.2 us
    ppermute x4, starting transfers between devices, all_gather(): cur_ccw = lax.ppermute(cur_ccw, 'rep', ccw)  13 us
    ppermute x4, waiting for transfers between devices, reduce_scatter(): got_ccw = lax.ppermute(send_ccw, 'rep', ccw)  10.8 us
    all_to_all x1, waiting for transfers between devices, on_device(): lax.all_to_all(spread, 'fsdp', 0, 0, tiled=False)  6.02 us
    all_to_all x1, starting transfers between devices, on_device(): lax.all_to_all(spread, 'fsdp', 0, 0, tiled=False)  5.21 us
    ppermute x1, waiting for transfers between devices, reduce_scatter(): return f32(total) + f32(lax.ppermute(total, 'rep', xp))  4.45 us
    convert_element_type x2, other arithmetic, term(): return (a - b.astype(jnp.float32)).astype(jnp.bfloat16)  4.02 us
  transfers between devices with their start and end apart: 19, of which 10 were waited for; matrix products, arithmetic and copies ran while one was open for 7% of the time, Pallas kernels for 0%

profile of v5, /device:TPU:4, one launch (start us, length us, event | category | flops | bytes accessed | tf_op | source)
XLA Modules:
  0.0 94.0 jit_solution(13765182647847546679)
XLA Ops:
  0.7 1.2 %fusion.18 = (bf16[1,128,512]{2,1,0:T(8,128)(2,1)S(1)}, bf16[1,128,512]{2,1,0:T(8,128)(2,1)S(1)}) fusion(f32[2,8,128,512]{3,2,1,0:T(8,128)} %bitcast.112, s32[]{:T(128)S(6)} %add.240, s32[]{:T(128)S(6)} %select_n.143, bf16[2,8,128,512]{3,2,1,0:T(8,128)(2,1)} %bitcast.117, s32[]{:T(128)S(6)} %select_n.141), kind=kLoop, calls=%fused_computation.51 | loop fusion | flops 393216 | bytes 1048588 | tf_op jit(solution)/shard_map/slice | solution.py:40
  1.9 2.0 %collective-permute-start = (bf16[1,128,512]{2,1,0:T(8,128)(2,1)S(1)}, bf16[1,128,512]{2,1,0:T(8,128)(2,1)S(1)}, u32[]{:S(2)}, u32[]{:S(2)}) collective-permute-start(bf16[1,128,512]{2,1,0:T(8,128)(2,1)S(1)} %get-tuple-element.11), channel_id=1, source_target_pairs={{0,16},{16,32},{32,48},{48,64},{64,80},{80,96},{96,112},{112,0},{1... | collective-permute-start | bytes 393224 | tf_op jit(solution)/shard_map/ppermute | solution.py:42
  3.9 4.0 %collective-permute-start.4 = (bf16[1,128,512]{2,1,0:T(8,128)(2,1)S(1)}, bf16[1,128,512]{2,1,0:T(8,128)(2,1)S(1)}, u32[]{:S(2)}, u32[]{:S(2)}) collective-permute-start(bf16[1,128,512]{2,1,0:T(8,128)(2,1)S(1)} %get-tuple-element.16), channel_id=1, source_target_pairs={{0,112},{16,0},{32,16},{48,32},{64,48},{80,64},{96,80},{112,96},{1... | collective-permute-start | bytes 393224 | tf_op jit(solution)/shard_map/ppermute | solution.py:43
  7.9 2.8 %fusion.9 = (bf16[2,128,512]{2,1,0:T(8,128)(2,1)S(1)}, bf16[2,128,512]{2,1,0:T(8,128)(2,1)S(1)}, bf16[2,128,512]{2,1,0:T(8,128)(2,1)S(1)}, bf16[2,128,512]{2,1,0...) fusion(f32[2,8,128,512]{3,2,1,0:T(8,128)} %bitcast.113, s32[]{:T(128)S(6)} %select_n.139, ...), kind=kLoop, calls=%fused_computation.25 | loop fusion | flops 2359296 | bytes 6291480 | tf_op jit(solution)/shard_map/convert_element_type | solution.py:97
  10.8 0.0 collective-permute-done.4
  10.9 3.6 %collective-permute-start.5 = (bf16[2,128,512]{2,1,0:T(8,128)(2,1)S(1)}, bf16[2,128,512]{2,1,0:T(8,128)(2,1)S(1)}, u32[]{:S(2)}, u32[]{:S(2)}) collective-permute-start(bf16[2,128,512]{2,1,0:T(8,128)(2,1)S(1)} %pad_maximum_fusion.1), channel_id=1, source_target_pairs={{0,112},{16,0},{32,16},{48,32},{64,48},{80,64},{96,80},{112,96},{1... | collective-permute-start | bytes 786440 | tf_op jit(solution)/shard_map/ppermute | solution.py:43
  14.6 0.1 collective-permute-start.1
  14.7 4.5 %collective-permute-done.5 = bf16[2,128,512]{2,1,0:T(8,128)(2,1)S(1)} collective-permute-done((bf16[2,128,512]{2,1,0:T(8,128)(2,1)S(1)}, bf16[2,128,512]{2,1,0:T(8,128)(2,1)S(1)}, u32[]{:S(2)}, u32[]{:S(2)}) %collective-permute-start.5) | collective-permute-done | bytes 262176 | tf_op jit(solution)/shard_map/ppermute | solution.py:43
  19.2 0.1 add_convert_fusion.2
  19.2 0.0 copy-start.1
  19.3 3.8 %collective-permute-start.6 = (bf16[2,128,512]{2,1,0:T(8,128)(2,1)S(1)}, bf16[2,128,512]{2,1,0:T(8,128)(2,1)S(1)}, u32[]{:S(2)}, u32[]{:S(2)}) collective-permute-start(bf16[2,128,512]{2,1,0:T(8,128)(2,1)S(1)} %add_convert_fusion.2), channel_id=1, source_target_pairs={{0,112},{16,0},{32,16},{48,32},{64,48},{80,64},{96,80},{112,96},{1... | collective-permute-start | bytes 786440 | tf_op jit(solution)/shard_map/ppermute | solution.py:43
  23.0 0.1 add_convert_fusion.4
  23.1 0.1 collective-permute-start.2
  23.2 1.2 %fusion.8 = bf16[2,128,512]{2,1,0:T(8,128)(2,1)S(1)} fusion(f32[2,8,128,512]{3,2,1,0:T(8,128)} %bitcast.114, s32[]{:T(128)S(6)} %select_n.155, bf16[2,8,128,512]{3,2,1,0:T(8,128)(2,1)} %bitcast.119), kind=kLoop, calls=%fused_computation.24 | loop fusion | flops 393216 | bytes 1048580 | tf_op jit(solution)/shard_map/convert_element_type | solution.py:97
  24.4 2.5 %collective-permute-done.6 = bf16[2,128,512]{2,1,0:T(8,128)(2,1)S(1)} collective-permute-done((bf16[2,128,512]{2,1,0:T(8,128)(2,1)S(1)}, bf16[2,128,512]{2,1,0:T(8,128)(2,1)S(1)}, u32[]{:S(2)}, u32[]{:S(2)}) %collective-permute-start.6) | collective-permute-done | bytes 262176 | tf_op jit(solution)/shard_map/ppermute | solution.py:43
  26.9 0.1 add_convert_fusion.1
  27.0 3.8 %collective-permute-start.7 = (bf16[2,128,512]{2,1,0:T(8,128)(2,1)S(1)}, bf16[2,128,512]{2,1,0:T(8,128)(2,1)S(1)}, u32[]{:S(2)}, u32[]{:S(2)}) collective-permute-start(bf16[2,128,512]{2,1,0:T(8,128)(2,1)S(1)} %add_convert_fusion.1), channel_id=1, source_target_pairs={{0,112},{16,0},{32,16},{48,32},{64,48},{80,64},{96,80},{112,96},{1... | collective-permute-start | bytes 786440 | tf_op jit(solution)/shard_map/ppermute | solution.py:43
  30.8 0.0 collective-permute-done.2
  30.8 0.1 add_convert_fusion.3
  30.8 0.1 collective-permute-start.3
  30.9 3.7 %collective-permute-done.7 = bf16[2,128,512]{2,1,0:T(8,128)(2,1)S(1)} collective-permute-done((bf16[2,128,512]{2,1,0:T(8,128)(2,1)S(1)}, bf16[2,128,512]{2,1,0:T(8,128)(2,1)S(1)}, u32[]{:S(2)}, u32[]{:S(2)}) %collective-permute-start.7) | collective-permute-done | bytes 262176 | tf_op jit(solution)/shard_map/ppermute | solution.py:43
  34.6 3.8 %collective-permute-done.3 = bf16[2,128,512]{2,1,0:T(8,128)(2,1)S(1)} collective-permute-done((bf16[2,128,512]{2,1,0:T(8,128)(2,1)S(1)}, bf16[2,128,512]{2,1,0:T(8,128)(2,1)S(1)}, u32[]{:S(2)}, u32[]{:S(2)}) %collective-permute-start.3) | collective-permute-done | bytes 262176 | tf_op jit(solution)/shard_map/ppermute | solution.py:42
  38.5 0.1 add_convert_fusion
  38.6 0.6 collective-permute-start.8
  39.2 3.0 %collective-permute-start.9 = (f32[128,512]{1,0:T(8,128)S(1)}, f32[128,512]{1,0:T(8,128)S(1)}, u32[]{:S(2)}, u32[]{:S(2)}) collective-permute-start(f32[128,512]{1,0:T(8,128)S(1)} %copy-done.1), channel_id=1, source_target_pairs={{0,128},{16,144},{32,160},{48,176},{64,192},{80,208},{96,224},{112... | collective-permute-start | bytes 786440 | tf_op jit(solution)/shard_map/ppermute | solution.py:101
  42.2 4.5 %collective-permute-done.8 = bf16[2,128,512]{2,1,0:T(8,128)(2,1)S(1)} collective-permute-done((bf16[2,128,512]{2,1,0:T(8,128)(2,1)S(1)}, bf16[2,128,512]{2,1,0:T(8,128)(2,1)S(1)}, u32[]{:S(2)}, u32[]{:S(2)}) %collective-permute-start.8) | collective-permute-done | bytes 262176 | tf_op jit(solution)/shard_map/ppermute | solution.py:58
  46.7 0.2 multiply_reduce_fusion
  46.9 0.6 broadcast_in_dim.38
  47.5 5.2 %all-to-all-start = ((f32[16,2,128]{2,1,0:T(2,128)}), f32[16,2,128]{2,1,0:T(2,128)S(1)}, u32[]{:S(2)}, u32[]{:S(2)}) async-start(f32[16,2,128]{2,1,0:T(2,128)} %broadcast_in_dim.38), calls=%async_computation | async-start | bytes 32768 | tf_op jit(solution)/shard_map/all_to_all | solution.py:109
  52.8 6.0 %all-to-all-done = f32[16,2,128]{2,1,0:T(2,128)S(1)} async-done(((f32[16,2,128]{2,1,0:T(2,128)}), f32[16,2,128]{2,1,0:T(2,128)S(1)}, u32[]{:S(2)}, u32[]{:S(2)}) %all-to-all-start) | async-done | bytes 16416 | tf_op jit(solution)/shard_map/all_to_all | solution.py:109
  58.8 0.2 broadcast_in_dim.37
  59.0 1.3 %bitcast_dynamic-update-slice_fusion.6 = (bf16[2,8,128,512]{3,2,1,0:T(8,128)(2,1)S(1)}, bf16[2,128,512]{2,1,0:T(8,128)(2,1)S(1)}, f32[2,128,512]{2,1,0:T(8,128)S(1)}) fusion(bf16[2,8,128,512]{3,2,1,0:T(8,128)(2,1)S(1)} %broadcast_in_dim.37, s32[]{:T(128)S(6)} %select_n.139, f32[1,128,512]{2,1,0:T(8,128)S(1)} %get-tuple-element.31, ...), kind=kLoop, calls=%fused_computation.43 | loop fusion | flops 1572864 | bytes 2622472 | tf_op jit(solution)/shard_map/dynamic_update_slice | solution.py:68
  60.3 0.1 collective-permute-start.10
  60.4 3.2 %collective-permute-start.11 = (bf16[2,128,512]{2,1,0:T(8,128)(2,1)S(1)}, bf16[2,128,512]{2,1,0:T(8,128)(2,1)S(1)}, u32[]{:S(2)}, u32[]{:S(2)}) collective-permute-start(bf16[2,128,512]{2,1,0:T(8,128)(2,1)S(1)} %get-tuple-element.20), channel_id=1, source_target_pairs={{0,112},{16,0},{32,16},{48,32},{64,48},{80,64},{96,80},{112,96},{1... | collective-permute-start | bytes 786440 | tf_op jit(solution)/shard_map/ppermute | solution.py:77
  63.6 0.1 fusion
  63.7 0.7 dynamic-slice_bitcast_fusion
  64.5 0.7 dynamic-slice_bitcast_fusion.1
  65.2 4.7 %collective-permute-done.10 = bf16[2,128,512]{2,1,0:T(8,128)(2,1)S(1)} collective-permute-done((bf16[2,128,512]{2,1,0:T(8,128)(2,1)S(1)}, bf16[2,128,512]{2,1,0:T(8,128)(2,1)S(1)}, u32[]{:S(2)}, u32[]{:S(2)}) %collective-permute-start.10) | collective-permute-done | bytes 262176 | tf_op jit(solution)/shard_map/ppermute | solution.py:76
  69.9 0.0 collective-permute-start.12
  69.9 3.2 %collective-permute-start.13 = (bf16[2,128,512]{2,1,0:T(8,128)(2,1)S(1)}, bf16[2,128,512]{2,1,0:T(8,128)(2,1)S(1)}, u32[]{:S(2)}, u32[]{:S(2)}) collective-permute-start(bf16[2,128,512]{2,1,0:T(8,128)(2,1)S(1)} %collective-permute-done.11), channel_id=1, source_target_pairs={{0,112},{16,0},{32,16},{48,32},{64,48},{80,64},{96,80},{112,96},{1... | collective-permute-start | bytes 786440 | tf_op jit(solution)/shard_map/ppermute | solution.py:77
  73.2 5.4 %collective-permute-done.12 = bf16[2,128,512]{2,1,0:T(8,128)(2,1)S(1)} collective-permute-done((bf16[2,128,512]{2,1,0:T(8,128)(2,1)S(1)}, bf16[2,128,512]{2,1,0:T(8,128)(2,1)S(1)}, u32[]{:S(2)}, u32[]{:S(2)}) %collective-permute-start.12) | collective-permute-done | bytes 262176 | tf_op jit(solution)/shard_map/ppermute | solution.py:76
  78.6 3.2 %collective-permute-start.15 = (bf16[2,128,512]{2,1,0:T(8,128)(2,1)S(1)}, bf16[2,128,512]{2,1,0:T(8,128)(2,1)S(1)}, u32[]{:S(2)}, u32[]{:S(2)}) collective-permute-start(bf16[2,128,512]{2,1,0:T(8,128)(2,1)S(1)} %collective-permute-done.13), channel_id=1, source_target_pairs={{0,112},{16,0},{32,16},{48,32},{64,48},{80,64},{96,80},{112,96},{1... | collective-permute-start | bytes 786440 | tf_op jit(solution)/shard_map/ppermute | solution.py:77
  81.9 4.5 %collective-permute-done.14 = bf16[2,128,512]{2,1,0:T(8,128)(2,1)S(1)} collective-permute-done((bf16[2,128,512]{2,1,0:T(8,128)(2,1)S(1)}, bf16[2,128,512]{2,1,0:T(8,128)(2,1)S(1)}, u32[]{:S(2)}, u32[]{:S(2)}) %collective-permute-start.14) | collective-permute-done | bytes 262176 | tf_op jit(solution)/shard_map/ppermute | solution.py:76
  86.4 0.1 collective-permute-start.16
  86.5 3.3 %collective-permute-start.17 = (bf16[1,128,512]{2,1,0:T(8,128)(2,1)S(1)}, bf16[1,128,512]{2,1,0:T(8,128)(2,1)S(1)}, u32[]{:S(2)}, u32[]{:S(2)}) collective-permute-start(bf16[1,128,512]{2,1,0:T(8,128)(2,1)S(1)} %slice.51), channel_id=1, source_target_pairs={{0,112},{16,0},{32,16},{48,32},{64,48},{80,64},{96,80},{112,96},{1... | collective-permute-start | bytes 393224 | tf_op jit(solution)/shard_map/ppermute | solution.py:77
  89.9 2.8 %collective-permute-done.16 = bf16[1,128,512]{2,1,0:T(8,128)(2,1)S(1)} collective-permute-done((bf16[1,128,512]{2,1,0:T(8,128)(2,1)S(1)}, bf16[1,128,512]{2,1,0:T(8,128)(2,1)S(1)}, u32[]{:S(2)}, u32[]{:S(2)}) %collective-permute-start.16) | collective-permute-done | bytes 131104 | tf_op jit(solution)/shard_map/ppermute | solution.py:76
  92.7 0.0 copy-start
  92.7 1.3 %copy-done = bf16[2,8,128,512]{3,2,1,0:T(8,128)(2,1)} copy-done((bf16[2,8,128,512]{3,2,1,0:T(8,128)(2,1)}, bf16[2,8,128,512]{3,2,1,0:T(8,128)(2,1)S(1)}, u32[]{:S(2)}) %copy-start) | copy-done | bytes 2097176
  (28 shorter events, 0.4 us)
Async XLA Ops:
  1.9 12.6 %collective-permute-start = (bf16[1,128,512]{2,1,0:T(8,128)(2,1)S(1)}, bf16[1,128,512]{2,1,0:T(8,128)(2,1)S(1)}, u32[]{:S(2)}, u32[]{:S(2)}) collective-permute-start(bf16[1,128,512]{2,1,0:T(8,128)(2,1)S(1)} %get-tuple-element.11), channel_id=1, source_target_pairs={{0,16},{16,32},{32,48},{48,64},{64,80},{80,96},{96,112},{112,0},{1... | collective-permute-start | bytes 393224 | tf_op jit(solution)/shard_map/ppermute | solution.py:42
  3.9 6.9 %collective-permute-start.4 = (bf16[1,128,512]{2,1,0:T(8,128)(2,1)S(1)}, bf16[1,128,512]{2,1,0:T(8,128)(2,1)S(1)}, u32[]{:S(2)}, u32[]{:S(2)}) collective-permute-start(bf16[1,128,512]{2,1,0:T(8,128)(2,1)S(1)} %get-tuple-element.16), channel_id=1, source_target_pairs={{0,112},{16,0},{32,16},{48,32},{64,48},{80,64},{96,80},{112,96},{1... | collective-permute-start | bytes 393224 | tf_op jit(solution)/shard_map/ppermute | solution.py:43
  10.9 8.3 %collective-permute-start.5 = (bf16[2,128,512]{2,1,0:T(8,128)(2,1)S(1)}, bf16[2,128,512]{2,1,0:T(8,128)(2,1)S(1)}, u32[]{:S(2)}, u32[]{:S(2)}) collective-permute-start(bf16[2,128,512]{2,1,0:T(8,128)(2,1)S(1)} %pad_maximum_fusion.1), channel_id=1, source_target_pairs={{0,112},{16,0},{32,16},{48,32},{64,48},{80,64},{96,80},{112,96},{1... | collective-permute-start | bytes 786440 | tf_op jit(solution)/shard_map/ppermute | solution.py:43
  14.6 8.5 %collective-permute-start.1 = (bf16[2,128,512]{2,1,0:T(8,128)(2,1)S(1)}, bf16[2,128,512]{2,1,0:T(8,128)(2,1)S(1)}, u32[]{:S(2)}, u32[]{:S(2)}) collective-permute-start(bf16[2,128,512]{2,1,0:T(8,128)(2,1)S(1)} %pad_maximum_fusion), channel_id=1, source_target_pairs={{0,16},{16,32},{32,48},{48,64},{64,80},{80,96},{96,112},{112,0},{1... | collective-permute-start | bytes 786440 | tf_op jit(solution)/shard_map/ppermute | solution.py:42
  19.2 19.9 %copy-start.1 = (f32[128,512]{1,0:T(8,128)S(1)}, f32[128,512]{1,0:T(8,128)}, u32[]{:S(2)}) copy-start(f32[128,512]{1,0:T(8,128)} %param.5) | copy-start | bytes 786436
  19.3 7.7 %collective-permute-start.6 = (bf16[2,128,512]{2,1,0:T(8,128)(2,1)S(1)}, bf16[2,128,512]{2,1,0:T(8,128)(2,1)S(1)}, u32[]{:S(2)}, u32[]{:S(2)}) collective-permute-start(bf16[2,128,512]{2,1,0:T(8,128)(2,1)S(1)} %add_convert_fusion.2), channel_id=1, source_target_pairs={{0,112},{16,0},{32,16},{48,32},{64,48},{80,64},{96,80},{112,96},{1... | collective-permute-start | bytes 786440 | tf_op jit(solution)/shard_map/ppermute | solution.py:43
  23.1 7.7 %collective-permute-start.2 = (bf16[2,128,512]{2,1,0:T(8,128)(2,1)S(1)}, bf16[2,128,512]{2,1,0:T(8,128)(2,1)S(1)}, u32[]{:S(2)}, u32[]{:S(2)}) collective-permute-start(bf16[2,128,512]{2,1,0:T(8,128)(2,1)S(1)} %add_convert_fusion.4), channel_id=1, source_target_pairs={{0,16},{16,32},{32,48},{48,64},{64,80},{80,96},{96,112},{112,0},{1... | collective-permute-start | bytes 786440 | tf_op jit(solution)/shard_map/ppermute | solution.py:42
  27.0 7.7 %collective-permute-start.7 = (bf16[2,128,512]{2,1,0:T(8,128)(2,1)S(1)}, bf16[2,128,512]{2,1,0:T(8,128)(2,1)S(1)}, u32[]{:S(2)}, u32[]{:S(2)}) collective-permute-start(bf16[2,128,512]{2,1,0:T(8,128)(2,1)S(1)} %add_convert_fusion.1), channel_id=1, source_target_pairs={{0,112},{16,0},{32,16},{48,32},{64,48},{80,64},{96,80},{112,96},{1... | collective-permute-start | bytes 786440 | tf_op jit(solution)/shard_map/ppermute | solution.py:43
  30.8 7.7 %collective-permute-start.3 = (bf16[2,128,512]{2,1,0:T(8,128)(2,1)S(1)}, bf16[2,128,512]{2,1,0:T(8,128)(2,1)S(1)}, u32[]{:S(2)}, u32[]{:S(2)}) collective-permute-start(bf16[2,128,512]{2,1,0:T(8,128)(2,1)S(1)} %add_convert_fusion.3), channel_id=1, source_target_pairs={{0,16},{16,32},{32,48},{48,64},{64,80},{80,96},{96,112},{112,0},{1... | collective-permute-start | bytes 786440 | tf_op jit(solution)/shard_map/ppermute | solution.py:42
  38.6 8.1 %collective-permute-start.8 = (bf16[2,128,512]{2,1,0:T(8,128)(2,1)S(1)}, bf16[2,128,512]{2,1,0:T(8,128)(2,1)S(1)}, u32[]{:S(2)}, u32[]{:S(2)}) collective-permute-start(bf16[2,128,512]{2,1,0:T(8,128)(2,1)S(1)} %add_convert_fusion), channel_id=1, source_target_pairs={{0,128},{16,144},{32,160},{48,176},{64,192},{80,208},{96,224},{112... | collective-permute-start | bytes 786440 | tf_op jit(solution)/shard_map/ppermute | solution.py:58
  39.2 13.5 %collective-permute-start.9 = (f32[128,512]{1,0:T(8,128)S(1)}, f32[128,512]{1,0:T(8,128)S(1)}, u32[]{:S(2)}, u32[]{:S(2)}) collective-permute-start(f32[128,512]{1,0:T(8,128)S(1)} %copy-done.1), channel_id=1, source_target_pairs={{0,128},{16,144},{32,160},{48,176},{64,192},{80,208},{96,224},{112... | collective-permute-start | bytes 786440 | tf_op jit(solution)/shard_map/ppermute | solution.py:101
  47.5 11.3 %all-to-all-start = ((f32[16,2,128]{2,1,0:T(2,128)}), f32[16,2,128]{2,1,0:T(2,128)S(1)}, u32[]{:S(2)}, u32[]{:S(2)}) async-start(f32[16,2,128]{2,1,0:T(2,128)} %broadcast_in_dim.38), calls=%async_computation | async-start | bytes 32768 | tf_op jit(solution)/shard_map/all_to_all | solution.py:109
  60.3 9.6 %collective-permute-start.10 = (bf16[2,128,512]{2,1,0:T(8,128)(2,1)S(1)}, bf16[2,128,512]{2,1,0:T(8,128)(2,1)S(1)}, u32[]{:S(2)}, u32[]{:S(2)}) collective-permute-start(bf16[2,128,512]{2,1,0:T(8,128)(2,1)S(1)} %get-tuple-element.20), channel_id=1, source_target_pairs={{0,16},{16,32},{32,48},{48,64},{64,80},{80,96},{96,112},{112,0},{1... | collective-permute-start | bytes 786440 | tf_op jit(solution)/shard_map/ppermute | solution.py:76
  60.4 9.5 %collective-permute-start.11 = (bf16[2,128,512]{2,1,0:T(8,128)(2,1)S(1)}, bf16[2,128,512]{2,1,0:T(8,128)(2,1)S(1)}, u32[]{:S(2)}, u32[]{:S(2)}) collective-permute-start(bf16[2,128,512]{2,1,0:T(8,128)(2,1)S(1)} %get-tuple-element.20), channel_id=1, source_target_pairs={{0,112},{16,0},{32,16},{48,32},{64,48},{80,64},{96,80},{112,96},{1... | collective-permute-start | bytes 786440 | tf_op jit(solution)/shard_map/ppermute | solution.py:77
  69.9 8.7 %collective-permute-start.12 = (bf16[2,128,512]{2,1,0:T(8,128)(2,1)S(1)}, bf16[2,128,512]{2,1,0:T(8,128)(2,1)S(1)}, u32[]{:S(2)}, u32[]{:S(2)}) collective-permute-start(bf16[2,128,512]{2,1,0:T(8,128)(2,1)S(1)} %collective-permute-done.10), channel_id=1, source_target_pairs={{0,16},{16,32},{32,48},{48,64},{64,80},{80,96},{96,112},{112,0},{1... | collective-permute-start | bytes 786440 | tf_op jit(solution)/shard_map/ppermute | solution.py:76
  69.9 8.7 %collective-permute-start.13 = (bf16[2,128,512]{2,1,0:T(8,128)(2,1)S(1)}, bf16[2,128,512]{2,1,0:T(8,128)(2,1)S(1)}, u32[]{:S(2)}, u32[]{:S(2)}) collective-permute-start(bf16[2,128,512]{2,1,0:T(8,128)(2,1)S(1)} %collective-permute-done.11), channel_id=1, source_target_pairs={{0,112},{16,0},{32,16},{48,32},{64,48},{80,64},{96,80},{112,96},{1... | collective-permute-start | bytes 786440 | tf_op jit(solution)/shard_map/ppermute | solution.py:77
  78.6 7.8 %collective-permute-start.14 = (bf16[2,128,512]{2,1,0:T(8,128)(2,1)S(1)}, bf16[2,128,512]{2,1,0:T(8,128)(2,1)S(1)}, u32[]{:S(2)}, u32[]{:S(2)}) collective-permute-start(bf16[2,128,512]{2,1,0:T(8,128)(2,1)S(1)} %collective-permute-done.12), channel_id=1, source_target_pairs={{0,16},{16,32},{32,48},{48,64},{64,80},{80,96},{96,112},{112,0},{1... | collective-permute-start | bytes 786440 | tf_op jit(solution)/shard_map/ppermute | solution.py:76
  78.6 7.9 %collective-permute-start.15 = (bf16[2,128,512]{2,1,0:T(8,128)(2,1)S(1)}, bf16[2,128,512]{2,1,0:T(8,128)(2,1)S(1)}, u32[]{:S(2)}, u32[]{:S(2)}) collective-permute-start(bf16[2,128,512]{2,1,0:T(8,128)(2,1)S(1)} %collective-permute-done.13), channel_id=1, source_target_pairs={{0,112},{16,0},{32,16},{48,32},{64,48},{80,64},{96,80},{112,96},{1... | collective-permute-start | bytes 786440 | tf_op jit(solution)/shard_map/ppermute | solution.py:77
  86.4 6.3 %collective-permute-start.16 = (bf16[1,128,512]{2,1,0:T(8,128)(2,1)S(1)}, bf16[1,128,512]{2,1,0:T(8,128)(2,1)S(1)}, u32[]{:S(2)}, u32[]{:S(2)}) collective-permute-start(bf16[1,128,512]{2,1,0:T(8,128)(2,1)S(1)} %slice.50), channel_id=1, source_target_pairs={{0,16},{16,32},{32,48},{48,64},{64,80},{80,96},{96,112},{112,0},{1... | collective-permute-start | bytes 393224 | tf_op jit(solution)/shard_map/ppermute | solution.py:76
  86.5 6.2 %collective-permute-start.17 = (bf16[1,128,512]{2,1,0:T(8,128)(2,1)S(1)}, bf16[1,128,512]{2,1,0:T(8,128)(2,1)S(1)}, u32[]{:S(2)}, u32[]{:S(2)}) collective-permute-start(bf16[1,128,512]{2,1,0:T(8,128)(2,1)S(1)} %slice.51), channel_id=1, source_target_pairs={{0,112},{16,0},{32,16},{48,32},{64,48},{80,64},{96,80},{112,96},{1... | collective-permute-start | bytes 393224 | tf_op jit(solution)/shard_map/ppermute | solution.py:77
  92.7 1.3 %copy-start = (bf16[2,8,128,512]{3,2,1,0:T(8,128)(2,1)}, bf16[2,8,128,512]{3,2,1,0:T(8,128)(2,1)S(1)}, u32[]{:S(2)}) copy-start(bf16[2,8,128,512]{3,2,1,0:T(8,128)(2,1)S(1)} %bitcast_dynamic-update-slice_fusion.7) | copy-start | bytes 6291460

commit v6 on v5

--- a/solution.py
+++ b/solution.py
@@ -111,7 +111,7 @@
     clipped = outer_grad * factor[..., None]
     both_new_momentum = momentum_coef * both_momentum + clipped
     both_new_master = both_outer - outer_rate * (clipped + momentum_coef * both_new_momentum)
-    new_weights = all_gather(both_new_master.astype(jnp.bfloat16), replicas)
+    new_weights = all_gather(lax.optimization_barrier(both_new_master.astype(jnp.bfloat16)), replicas)
     new_master = lax.dynamic_index_in_dim(both_new_master, xh, 0, keepdims=False)
     new_momentum = lax.dynamic_index_in_dim(both_new_momentum, xh, 0, keepdims=False)
     return (new_weights, new_master, new_momentum)

time: 94.3 us -> 92.7 us (0.983)
  starting transfers between devices: 39.4 us -> 38.1 us
    ppermute x4, waiting for transfers between devices: 10.8 us -> 0.01 us  [reduce_scatter(): got_ccw = lax.ppermute(send_ccw, 'rep', ccw)]
    ppermute x4, waiting for transfers between devices: 3.86 us -> 13.3 us  [reduce_scatter(): got_cw = lax.ppermute(send_cw, 'rep', cw)]
    ppermute x4, starting transfers between devices: 15.2 us -> 13.9 us  [reduce_scatter(): got_ccw = lax.ppermute(send_ccw, 'rep', ccw)]
    dynamic_update_slice x1 -> x0, other arithmetic: 1.27 us -> none  [all_gather(): lax.dynamic_update_slice(o, piece[:, None], (row, pos % nz, 0, 0))]
    convert_element_type x0 -> x1, other arithmetic: none -> 1.26 us  [on_device(): both_new_master.astype(jnp.bfloat16)]
    ppermute x4, waiting for transfers between devices: 17.4 us -> 18.4 us  [all_gather(): cur_cw = lax.ppermute(cur_cw, 'rep', cw)]
where the time goes in v6:
time: 92.7 us; the launch traced here: 92.5 us
  waiting for transfers between devices  43 us (46%)
  starting transfers between devices  38.1 us (41%)
  other arithmetic  7.2 us (8%)
  local copies, waits for them, and re-layouts  3.18 us (3%)
  between operations  0.98 us (1%)
    ppermute x4, waiting for transfers between devices, all_gather(): cur_cw = lax.ppermute(cur_cw, 'rep', cw)  18.4 us
    ppermute x4, starting transfers between devices, reduce_scatter(): got_ccw = lax.ppermute(send_ccw, 'rep', ccw)  13.9 us
    ppermute x4, waiting for transfers between devices, reduce_scatter(): got_cw = lax.ppermute(send_cw, 'rep', cw)  13.3 us
    ppermute x4, starting transfers between devices, all_gather(): cur_ccw = lax.ppermute(cur_ccw, 'rep', ccw)  13 us
    all_to_all x1, waiting for transfers between devices, on_device(): lax.all_to_all(spread, 'fsdp', 0, 0, tiled=False)  6.02 us
    ppermute x1, waiting for transfers between devices, reduce_scatter(): return f32(total) + f32(lax.ppermute(total, 'rep', xp))  5.28 us
    all_to_all x1, starting transfers between devices, on_device(): lax.all_to_all(spread, 'fsdp', 0, 0, tiled=False)  5.21 us
    convert_element_type x2, other arithmetic, term(): return (a - b.astype(jnp.float32)).astype(jnp.bfloat16)  4.01 us
  transfers between devices with their start and end apart: 19, of which 10 were waited for; matrix products, arithmetic and copies ran while one was open for 7% of the time, Pallas kernels for 0%

profile of v6, /device:TPU:4, one launch (start us, length us, event | category | flops | bytes accessed | tf_op | source)
XLA Modules:
  0.0 92.5 jit_solution(6352439781814943217)
XLA Ops:
  0.7 1.2 %fusion.18 = (bf16[1,128,512]{2,1,0:T(8,128)(2,1)S(1)}, bf16[1,128,512]{2,1,0:T(8,128)(2,1)S(1)}) fusion(f32[2,8,128,512]{3,2,1,0:T(8,128)} %bitcast.112, s32[]{:T(128)S(6)} %add.240, s32[]{:T(128)S(6)} %select_n.143, bf16[2,8,128,512]{3,2,1,0:T(8,128)(2,1)} %bitcast.117, s32[]{:T(128)S(6)} %select_n.141), kind=kLoop, calls=%fused_computation.51 | loop fusion | flops 393216 | bytes 1048588 | tf_op jit(solution)/shard_map/slice | solution.py:40
  1.9 2.0 %collective-permute-start = (bf16[1,128,512]{2,1,0:T(8,128)(2,1)S(1)}, bf16[1,128,512]{2,1,0:T(8,128)(2,1)S(1)}, u32[]{:S(2)}, u32[]{:S(2)}) collective-permute-start(bf16[1,128,512]{2,1,0:T(8,128)(2,1)S(1)} %get-tuple-element.11), channel_id=1, source_target_pairs={{0,16},{16,32},{32,48},{48,64},{64,80},{80,96},{96,112},{112,0},{1... | collective-permute-start | bytes 393224 | tf_op jit(solution)/shard_map/ppermute | solution.py:42
  3.9 4.0 %collective-permute-start.4 = (bf16[1,128,512]{2,1,0:T(8,128)(2,1)S(1)}, bf16[1,128,512]{2,1,0:T(8,128)(2,1)S(1)}, u32[]{:S(2)}, u32[]{:S(2)}) collective-permute-start(bf16[1,128,512]{2,1,0:T(8,128)(2,1)S(1)} %get-tuple-element.16), channel_id=1, source_target_pairs={{0,112},{16,0},{32,16},{48,32},{64,48},{80,64},{96,80},{112,96},{1... | collective-permute-start | bytes 393224 | tf_op jit(solution)/shard_map/ppermute | solution.py:43
  7.9 2.8 %fusion.9 = (bf16[2,128,512]{2,1,0:T(8,128)(2,1)S(1)}, bf16[2,128,512]{2,1,0:T(8,128)(2,1)S(1)}, bf16[2,128,512]{2,1,0:T(8,128)(2,1)S(1)}, bf16[2,128,512]{2,1,0...) fusion(f32[2,8,128,512]{3,2,1,0:T(8,128)} %bitcast.113, s32[]{:T(128)S(6)} %select_n.139, ...), kind=kLoop, calls=%fused_computation.25 | loop fusion | flops 2359296 | bytes 6291480 | tf_op jit(solution)/shard_map/convert_element_type | solution.py:97
  10.8 0.5 collective-permute-done
  11.4 0.1 collective-permute-start.1
  11.5 0.0 collective-permute-done.4
  11.5 3.3 %collective-permute-start.5 = (bf16[2,128,512]{2,1,0:T(8,128)(2,1)S(1)}, bf16[2,128,512]{2,1,0:T(8,128)(2,1)S(1)}, u32[]{:S(2)}, u32[]{:S(2)}) collective-permute-start(bf16[2,128,512]{2,1,0:T(8,128)(2,1)S(1)} %pad_maximum_fusion.1), channel_id=1, source_target_pairs={{0,112},{16,0},{32,16},{48,32},{64,48},{80,64},{96,80},{112,96},{1... | collective-permute-start | bytes 786440 | tf_op jit(solution)/shard_map/ppermute | solution.py:43
  14.8 5.3 %collective-permute-done.1 = bf16[2,128,512]{2,1,0:T(8,128)(2,1)S(1)} collective-permute-done((bf16[2,128,512]{2,1,0:T(8,128)(2,1)S(1)}, bf16[2,128,512]{2,1,0:T(8,128)(2,1)S(1)}, u32[]{:S(2)}, u32[]{:S(2)}) %collective-permute-start.1) | collective-permute-done | bytes 262176 | tf_op jit(solution)/shard_map/ppermute | solution.py:42
  20.2 0.1 add_convert_fusion.4
  20.2 0.0 copy-start.1
  20.2 0.1 collective-permute-start.2
  20.3 0.1 add_convert_fusion.2
  20.4 3.3 %collective-permute-start.6 = (bf16[2,128,512]{2,1,0:T(8,128)(2,1)S(1)}, bf16[2,128,512]{2,1,0:T(8,128)(2,1)S(1)}, u32[]{:S(2)}, u32[]{:S(2)}) collective-permute-start(bf16[2,128,512]{2,1,0:T(8,128)(2,1)S(1)} %add_convert_fusion.2), channel_id=1, source_target_pairs={{0,112},{16,0},{32,16},{48,32},{64,48},{80,64},{96,80},{112,96},{1... | collective-permute-start | bytes 786440 | tf_op jit(solution)/shard_map/ppermute | solution.py:43
  23.7 1.2 %fusion.8 = bf16[2,128,512]{2,1,0:T(8,128)(2,1)S(1)} fusion(f32[2,8,128,512]{3,2,1,0:T(8,128)} %bitcast.114, s32[]{:T(128)S(6)} %select_n.155, bf16[2,8,128,512]{3,2,1,0:T(8,128)(2,1)} %bitcast.119), kind=kLoop, calls=%fused_computation.24 | loop fusion | flops 393216 | bytes 1048580 | tf_op jit(solution)/shard_map/convert_element_type | solution.py:97
  24.9 3.2 %collective-permute-done.2 = bf16[2,128,512]{2,1,0:T(8,128)(2,1)S(1)} collective-permute-done((bf16[2,128,512]{2,1,0:T(8,128)(2,1)S(1)}, bf16[2,128,512]{2,1,0:T(8,128)(2,1)S(1)}, u32[]{:S(2)}, u32[]{:S(2)}) %collective-permute-start.2) | collective-permute-done | bytes 262176 | tf_op jit(solution)/shard_map/ppermute | solution.py:42
  28.1 0.1 add_convert_fusion.3
  28.2 0.1 collective-permute-start.3
  28.3 0.0 collective-permute-done.6
  28.3 0.1 add_convert_fusion.1
  28.3 3.3 %collective-permute-start.7 = (bf16[2,128,512]{2,1,0:T(8,128)(2,1)S(1)}, bf16[2,128,512]{2,1,0:T(8,128)(2,1)S(1)}, u32[]{:S(2)}, u32[]{:S(2)}) collective-permute-start(bf16[2,128,512]{2,1,0:T(8,128)(2,1)S(1)} %add_convert_fusion.1), channel_id=1, source_target_pairs={{0,112},{16,0},{32,16},{48,32},{64,48},{80,64},{96,80},{112,96},{1... | collective-permute-start | bytes 786440 | tf_op jit(solution)/shard_map/ppermute | solution.py:43
  31.6 4.2 %collective-permute-done.3 = bf16[2,128,512]{2,1,0:T(8,128)(2,1)S(1)} collective-permute-done((bf16[2,128,512]{2,1,0:T(8,128)(2,1)S(1)}, bf16[2,128,512]{2,1,0:T(8,128)(2,1)S(1)}, u32[]{:S(2)}, u32[]{:S(2)}) %collective-permute-start.3) | collective-permute-done | bytes 262176 | tf_op jit(solution)/shard_map/ppermute | solution.py:42
  35.8 0.1 add_convert_fusion
  35.9 0.6 collective-permute-start.8
  36.5 3.0 %collective-permute-start.9 = (f32[128,512]{1,0:T(8,128)S(1)}, f32[128,512]{1,0:T(8,128)S(1)}, u32[]{:S(2)}, u32[]{:S(2)}) collective-permute-start(f32[128,512]{1,0:T(8,128)S(1)} %copy-done.1), channel_id=1, source_target_pairs={{0,128},{16,144},{32,160},{48,176},{64,192},{80,208},{96,224},{112... | collective-permute-start | bytes 786440 | tf_op jit(solution)/shard_map/ppermute | solution.py:101
  39.6 5.3 %collective-permute-done.8 = bf16[2,128,512]{2,1,0:T(8,128)(2,1)S(1)} collective-permute-done((bf16[2,128,512]{2,1,0:T(8,128)(2,1)S(1)}, bf16[2,128,512]{2,1,0:T(8,128)(2,1)S(1)}, u32[]{:S(2)}, u32[]{:S(2)}) %collective-permute-start.8) | collective-permute-done | bytes 262176 | tf_op jit(solution)/shard_map/ppermute | solution.py:58
  44.8 0.2 multiply_reduce_fusion
  45.0 0.6 broadcast_in_dim.38
  45.6 5.2 %all-to-all-start = ((f32[16,2,128]{2,1,0:T(2,128)}), f32[16,2,128]{2,1,0:T(2,128)S(1)}, u32[]{:S(2)}, u32[]{:S(2)}) async-start(f32[16,2,128]{2,1,0:T(2,128)} %broadcast_in_dim.38), calls=%async_computation | async-start | bytes 32768 | tf_op jit(solution)/shard_map/all_to_all | solution.py:109
  50.8 0.0 collective-permute-done.9
  50.9 6.0 %all-to-all-done = f32[16,2,128]{2,1,0:T(2,128)S(1)} async-done(((f32[16,2,128]{2,1,0:T(2,128)}), f32[16,2,128]{2,1,0:T(2,128)S(1)}, u32[]{:S(2)}, u32[]{:S(2)}) %all-to-all-start) | async-done | bytes 16416 | tf_op jit(solution)/shard_map/all_to_all | solution.py:109
  57.0 1.3 %fusion.19 = (bf16[2,128,512]{2,1,0:T(8,128)(2,1)S(1)}, f32[2,128,512]{2,1,0:T(8,128)S(1)}, f32[2,128,512]{2,1,0:T(8,128)S(1)}) fusion(f32[1,128,512]{2,1,0:T(8,128)S(1)} %get-tuple-element.31, f32[1,128,512]{2,1,0:T(8,128)S(1)} %get-tuple-element.30, f32[2,128]{1,0:T(2,128)S(1)} %minimum_multiply_fusion, ...), kind=kLoop, calls=%fused_computation.55 | loop fusion | flops 1572864 | bytes 2884612 | tf_op jit(solution)/shard_map/convert_element_type | solution.py:114
  58.2 0.1 collective-permute-start.10
  58.3 3.2 %collective-permute-start.11 = (bf16[2,128,512]{2,1,0:T(8,128)(2,1)S(1)}, bf16[2,128,512]{2,1,0:T(8,128)(2,1)S(1)}, u32[]{:S(2)}, u32[]{:S(2)}) collective-permute-start(bf16[2,128,512]{2,1,0:T(8,128)(2,1)S(1)} %get-tuple-element.19), channel_id=1, source_target_pairs={{0,112},{16,0},{32,16},{48,32},{64,48},{80,64},{96,80},{112,96},{1... | collective-permute-start | bytes 786440 | tf_op jit(solution)/shard_map/ppermute | solution.py:77
  61.5 0.8 dynamic-slice_bitcast_fusion
  62.4 0.2 broadcast_in_dim.37
  62.6 5.4 %collective-permute-done.10 = bf16[2,128,512]{2,1,0:T(8,128)(2,1)S(1)} collective-permute-done((bf16[2,128,512]{2,1,0:T(8,128)(2,1)S(1)}, bf16[2,128,512]{2,1,0:T(8,128)(2,1)S(1)}, u32[]{:S(2)}, u32[]{:S(2)}) %collective-permute-start.10) | collective-permute-done | bytes 262176 | tf_op jit(solution)/shard_map/ppermute | solution.py:76
  68.0 0.0 collective-permute-start.12
  68.0 0.0 collective-permute-done.11
  68.0 3.2 %collective-permute-start.13 = (bf16[2,128,512]{2,1,0:T(8,128)(2,1)S(1)}, bf16[2,128,512]{2,1,0:T(8,128)(2,1)S(1)}, u32[]{:S(2)}, u32[]{:S(2)}) collective-permute-start(bf16[2,128,512]{2,1,0:T(8,128)(2,1)S(1)} %collective-permute-done.11), channel_id=1, source_target_pairs={{0,112},{16,0},{32,16},{48,32},{64,48},{80,64},{96,80},{112,96},{1... | collective-permute-start | bytes 786440 | tf_op jit(solution)/shard_map/ppermute | solution.py:77
  71.3 5.6 %collective-permute-done.12 = bf16[2,128,512]{2,1,0:T(8,128)(2,1)S(1)} collective-permute-done((bf16[2,128,512]{2,1,0:T(8,128)(2,1)S(1)}, bf16[2,128,512]{2,1,0:T(8,128)(2,1)S(1)}, u32[]{:S(2)}, u32[]{:S(2)}) %collective-permute-start.12) | collective-permute-done | bytes 262176 | tf_op jit(solution)/shard_map/ppermute | solution.py:76
  76.9 3.2 %collective-permute-start.15 = (bf16[2,128,512]{2,1,0:T(8,128)(2,1)S(1)}, bf16[2,128,512]{2,1,0:T(8,128)(2,1)S(1)}, u32[]{:S(2)}, u32[]{:S(2)}) collective-permute-start(bf16[2,128,512]{2,1,0:T(8,128)(2,1)S(1)} %collective-permute-done.13), channel_id=1, source_target_pairs={{0,112},{16,0},{32,16},{48,32},{64,48},{80,64},{96,80},{112,96},{1... | collective-permute-start | bytes 786440 | tf_op jit(solution)/shard_map/ppermute | solution.py:77
  80.2 4.7 %collective-permute-done.14 = bf16[2,128,512]{2,1,0:T(8,128)(2,1)S(1)} collective-permute-done((bf16[2,128,512]{2,1,0:T(8,128)(2,1)S(1)}, bf16[2,128,512]{2,1,0:T(8,128)(2,1)S(1)}, u32[]{:S(2)}, u32[]{:S(2)}) %collective-permute-start.14) | collective-permute-done | bytes 262176 | tf_op jit(solution)/shard_map/ppermute | solution.py:76
  84.8 0.1 collective-permute-start.16
  85.0 3.3 %collective-permute-start.17 = (bf16[1,128,512]{2,1,0:T(8,128)(2,1)S(1)}, bf16[1,128,512]{2,1,0:T(8,128)(2,1)S(1)}, u32[]{:S(2)}, u32[]{:S(2)}) collective-permute-start(bf16[1,128,512]{2,1,0:T(8,128)(2,1)S(1)} %slice.51), channel_id=1, source_target_pairs={{0,112},{16,0},{32,16},{48,32},{64,48},{80,64},{96,80},{112,96},{1... | collective-permute-start | bytes 393224 | tf_op jit(solution)/shard_map/ppermute | solution.py:77
  88.3 2.8 %collective-permute-done.16 = bf16[1,128,512]{2,1,0:T(8,128)(2,1)S(1)} collective-permute-done((bf16[1,128,512]{2,1,0:T(8,128)(2,1)S(1)}, bf16[1,128,512]{2,1,0:T(8,128)(2,1)S(1)}, u32[]{:S(2)}, u32[]{:S(2)}) %collective-permute-start.16) | collective-permute-done | bytes 131104 | tf_op jit(solution)/shard_map/ppermute | solution.py:76
  91.1 0.0 copy-start
  91.2 1.3 %copy-done = bf16[2,8,128,512]{3,2,1,0:T(8,128)(2,1)} copy-done((bf16[2,8,128,512]{3,2,1,0:T(8,128)(2,1)}, bf16[2,8,128,512]{3,2,1,0:T(8,128)(2,1)S(1)}, u32[]{:S(2)}) %copy-start) | copy-done | bytes 2097176
  (27 shorter events, 0.5 us)
Async XLA Ops:
  1.9 9.4 %collective-permute-start = (bf16[1,128,512]{2,1,0:T(8,128)(2,1)S(1)}, bf16[1,128,512]{2,1,0:T(8,128)(2,1)S(1)}, u32[]{:S(2)}, u32[]{:S(2)}) collective-permute-start(bf16[1,128,512]{2,1,0:T(8,128)(2,1)S(1)} %get-tuple-element.11), channel_id=1, source_target_pairs={{0,16},{16,32},{32,48},{48,64},{64,80},{80,96},{96,112},{112,0},{1... | collective-permute-start | bytes 393224 | tf_op jit(solution)/shard_map/ppermute | solution.py:42
  3.9 7.6 %collective-permute-start.4 = (bf16[1,128,512]{2,1,0:T(8,128)(2,1)S(1)}, bf16[1,128,512]{2,1,0:T(8,128)(2,1)S(1)}, u32[]{:S(2)}, u32[]{:S(2)}) collective-permute-start(bf16[1,128,512]{2,1,0:T(8,128)(2,1)S(1)} %get-tuple-element.16), channel_id=1, source_target_pairs={{0,112},{16,0},{32,16},{48,32},{64,48},{80,64},{96,80},{112,96},{1... | collective-permute-start | bytes 393224 | tf_op jit(solution)/shard_map/ppermute | solution.py:43
  11.4 8.8 %collective-permute-start.1 = (bf16[2,128,512]{2,1,0:T(8,128)(2,1)S(1)}, bf16[2,128,512]{2,1,0:T(8,128)(2,1)S(1)}, u32[]{:S(2)}, u32[]{:S(2)}) collective-permute-start(bf16[2,128,512]{2,1,0:T(8,128)(2,1)S(1)} %pad_maximum_fusion), channel_id=1, source_target_pairs={{0,16},{16,32},{32,48},{48,64},{64,80},{80,96},{96,112},{112,0},{1... | collective-permute-start | bytes 786440 | tf_op jit(solution)/shard_map/ppermute | solution.py:42
  11.5 8.8 %collective-permute-start.5 = (bf16[2,128,512]{2,1,0:T(8,128)(2,1)S(1)}, bf16[2,128,512]{2,1,0:T(8,128)(2,1)S(1)}, u32[]{:S(2)}, u32[]{:S(2)}) collective-permute-start(bf16[2,128,512]{2,1,0:T(8,128)(2,1)S(1)} %pad_maximum_fusion.1), channel_id=1, source_target_pairs={{0,112},{16,0},{32,16},{48,32},{64,48},{80,64},{96,80},{112,96},{1... | collective-permute-start | bytes 786440 | tf_op jit(solution)/shard_map/ppermute | solution.py:43
  20.2 16.3 %copy-start.1 = (f32[128,512]{1,0:T(8,128)S(1)}, f32[128,512]{1,0:T(8,128)}, u32[]{:S(2)}) copy-start(f32[128,512]{1,0:T(8,128)} %param.5) | copy-start | bytes 786436
  20.2 7.9 %collective-permute-start.2 = (bf16[2,128,512]{2,1,0:T(8,128)(2,1)S(1)}, bf16[2,128,512]{2,1,0:T(8,128)(2,1)S(1)}, u32[]{:S(2)}, u32[]{:S(2)}) collective-permute-start(bf16[2,128,512]{2,1,0:T(8,128)(2,1)S(1)} %add_convert_fusion.4), channel_id=1, source_target_pairs={{0,16},{16,32},{32,48},{48,64},{64,80},{80,96},{96,112},{112,0},{1... | collective-permute-start | bytes 786440 | tf_op jit(solution)/shard_map/ppermute | solution.py:42
  20.4 7.8 %collective-permute-start.6 = (bf16[2,128,512]{2,1,0:T(8,128)(2,1)S(1)}, bf16[2,128,512]{2,1,0:T(8,128)(2,1)S(1)}, u32[]{:S(2)}, u32[]{:S(2)}) collective-permute-start(bf16[2,128,512]{2,1,0:T(8,128)(2,1)S(1)} %add_convert_fusion.2), channel_id=1, source_target_pairs={{0,112},{16,0},{32,16},{48,32},{64,48},{80,64},{96,80},{112,96},{1... | collective-permute-start | bytes 786440 | tf_op jit(solution)/shard_map/ppermute | solution.py:43
  28.2 7.7 %collective-permute-start.3 = (bf16[2,128,512]{2,1,0:T(8,128)(2,1)S(1)}, bf16[2,128,512]{2,1,0:T(8,128)(2,1)S(1)}, u32[]{:S(2)}, u32[]{:S(2)}) collective-permute-start(bf16[2,128,512]{2,1,0:T(8,128)(2,1)S(1)} %add_convert_fusion.3), channel_id=1, source_target_pairs={{0,16},{16,32},{32,48},{48,64},{64,80},{80,96},{96,112},{112,0},{1... | collective-permute-start | bytes 786440 | tf_op jit(solution)/shard_map/ppermute | solution.py:42
  28.3 7.5 %collective-permute-start.7 = (bf16[2,128,512]{2,1,0:T(8,128)(2,1)S(1)}, bf16[2,128,512]{2,1,0:T(8,128)(2,1)S(1)}, u32[]{:S(2)}, u32[]{:S(2)}) collective-permute-start(bf16[2,128,512]{2,1,0:T(8,128)(2,1)S(1)} %add_convert_fusion.1), channel_id=1, source_target_pairs={{0,112},{16,0},{32,16},{48,32},{64,48},{80,64},{96,80},{112,96},{1... | collective-permute-start | bytes 786440 | tf_op jit(solution)/shard_map/ppermute | solution.py:43
  35.9 8.9 %collective-permute-start.8 = (bf16[2,128,512]{2,1,0:T(8,128)(2,1)S(1)}, bf16[2,128,512]{2,1,0:T(8,128)(2,1)S(1)}, u32[]{:S(2)}, u32[]{:S(2)}) collective-permute-start(bf16[2,128,512]{2,1,0:T(8,128)(2,1)S(1)} %add_convert_fusion), channel_id=1, source_target_pairs={{0,128},{16,144},{32,160},{48,176},{64,192},{80,208},{96,224},{112... | collective-permute-start | bytes 786440 | tf_op jit(solution)/shard_map/ppermute | solution.py:58
  36.5 14.3 %collective-permute-start.9 = (f32[128,512]{1,0:T(8,128)S(1)}, f32[128,512]{1,0:T(8,128)S(1)}, u32[]{:S(2)}, u32[]{:S(2)}) collective-permute-start(f32[128,512]{1,0:T(8,128)S(1)} %copy-done.1), channel_id=1, source_target_pairs={{0,128},{16,144},{32,160},{48,176},{64,192},{80,208},{96,224},{112... | collective-permute-start | bytes 786440 | tf_op jit(solution)/shard_map/ppermute | solution.py:101
  45.6 11.3 %all-to-all-start = ((f32[16,2,128]{2,1,0:T(2,128)}), f32[16,2,128]{2,1,0:T(2,128)S(1)}, u32[]{:S(2)}, u32[]{:S(2)}) async-start(f32[16,2,128]{2,1,0:T(2,128)} %broadcast_in_dim.38), calls=%async_computation | async-start | bytes 32768 | tf_op jit(solution)/shard_map/all_to_all | solution.py:109
  58.2 9.8 %collective-permute-start.10 = (bf16[2,128,512]{2,1,0:T(8,128)(2,1)S(1)}, bf16[2,128,512]{2,1,0:T(8,128)(2,1)S(1)}, u32[]{:S(2)}, u32[]{:S(2)}) collective-permute-start(bf16[2,128,512]{2,1,0:T(8,128)(2,1)S(1)} %get-tuple-element.19), channel_id=1, source_target_pairs={{0,16},{16,32},{32,48},{48,64},{64,80},{80,96},{96,112},{112,0},{1... | collective-permute-start | bytes 786440 | tf_op jit(solution)/shard_map/ppermute | solution.py:76
  58.3 9.7 %collective-permute-start.11 = (bf16[2,128,512]{2,1,0:T(8,128)(2,1)S(1)}, bf16[2,128,512]{2,1,0:T(8,128)(2,1)S(1)}, u32[]{:S(2)}, u32[]{:S(2)}) collective-permute-start(bf16[2,128,512]{2,1,0:T(8,128)(2,1)S(1)} %get-tuple-element.19), channel_id=1, source_target_pairs={{0,112},{16,0},{32,16},{48,32},{64,48},{80,64},{96,80},{112,96},{1... | collective-permute-start | bytes 786440 | tf_op jit(solution)/shard_map/ppermute | solution.py:77
  68.0 8.9 %collective-permute-start.12 = (bf16[2,128,512]{2,1,0:T(8,128)(2,1)S(1)}, bf16[2,128,512]{2,1,0:T(8,128)(2,1)S(1)}, u32[]{:S(2)}, u32[]{:S(2)}) collective-permute-start(bf16[2,128,512]{2,1,0:T(8,128)(2,1)S(1)} %collective-permute-done.10), channel_id=1, source_target_pairs={{0,16},{16,32},{32,48},{48,64},{64,80},{80,96},{96,112},{112,0},{1... | collective-permute-start | bytes 786440 | tf_op jit(solution)/shard_map/ppermute | solution.py:76
  68.0 8.9 %collective-permute-start.13 = (bf16[2,128,512]{2,1,0:T(8,128)(2,1)S(1)}, bf16[2,128,512]{2,1,0:T(8,128)(2,1)S(1)}, u32[]{:S(2)}, u32[]{:S(2)}) collective-permute-start(bf16[2,128,512]{2,1,0:T(8,128)(2,1)S(1)} %collective-permute-done.11), channel_id=1, source_target_pairs={{0,112},{16,0},{32,16},{48,32},{64,48},{80,64},{96,80},{112,96},{1... | collective-permute-start | bytes 786440 | tf_op jit(solution)/shard_map/ppermute | solution.py:77
  76.9 8.0 %collective-permute-start.14 = (bf16[2,128,512]{2,1,0:T(8,128)(2,1)S(1)}, bf16[2,128,512]{2,1,0:T(8,128)(2,1)S(1)}, u32[]{:S(2)}, u32[]{:S(2)}) collective-permute-start(bf16[2,128,512]{2,1,0:T(8,128)(2,1)S(1)} %collective-permute-done.12), channel_id=1, source_target_pairs={{0,16},{16,32},{32,48},{48,64},{64,80},{80,96},{96,112},{112,0},{1... | collective-permute-start | bytes 786440 | tf_op jit(solution)/shard_map/ppermute | solution.py:76
  76.9 8.1 %collective-permute-start.15 = (bf16[2,128,512]{2,1,0:T(8,128)(2,1)S(1)}, bf16[2,128,512]{2,1,0:T(8,128)(2,1)S(1)}, u32[]{:S(2)}, u32[]{:S(2)}) collective-permute-start(bf16[2,128,512]{2,1,0:T(8,128)(2,1)S(1)} %collective-permute-done.13), channel_id=1, source_target_pairs={{0,112},{16,0},{32,16},{48,32},{64,48},{80,64},{96,80},{112,96},{1... | collective-permute-start | bytes 786440 | tf_op jit(solution)/shard_map/ppermute | solution.py:77
  84.8 6.3 %collective-permute-start.16 = (bf16[1,128,512]{2,1,0:T(8,128)(2,1)S(1)}, bf16[1,128,512]{2,1,0:T(8,128)(2,1)S(1)}, u32[]{:S(2)}, u32[]{:S(2)}) collective-permute-start(bf16[1,128,512]{2,1,0:T(8,128)(2,1)S(1)} %slice.50), channel_id=1, source_target_pairs={{0,16},{16,32},{32,48},{48,64},{64,80},{80,96},{96,112},{112,0},{1... | collective-permute-start | bytes 393224 | tf_op jit(solution)/shard_map/ppermute | solution.py:76
  85.0 6.2 %collective-permute-start.17 = (bf16[1,128,512]{2,1,0:T(8,128)(2,1)S(1)}, bf16[1,128,512]{2,1,0:T(8,128)(2,1)S(1)}, u32[]{:S(2)}, u32[]{:S(2)}) collective-permute-start(bf16[1,128,512]{2,1,0:T(8,128)(2,1)S(1)} %slice.51), channel_id=1, source_target_pairs={{0,112},{16,0},{32,16},{48,32},{64,48},{80,64},{96,80},{112,96},{1... | collective-permute-start | bytes 393224 | tf_op jit(solution)/shard_map/ppermute | solution.py:77
  91.1 1.3 %copy-start = (bf16[2,8,128,512]{3,2,1,0:T(8,128)(2,1)}, bf16[2,8,128,512]{3,2,1,0:T(8,128)(2,1)S(1)}, u32[]{:S(2)}) copy-start(bf16[2,8,128,512]{3,2,1,0:T(8,128)(2,1)S(1)} %bitcast_dynamic-update-slice_fusion.7) | copy-start | bytes 6291460
